TPU v7x, 128 devices: a whole 4x4x4 slice. The times are simulated.
128 devices in a mesh: lat: 8 (over y_lo, z), lon: 16 (over x, y_hi, core).
Axes of the slice: x: 4, y: 4 (y_hi: 2, y_lo: 2; y = y_hi * 2 + y_lo), z: 4, core: 2. Of those that a mesh axis runs over, the one named last changes fastest.
Arguments:
- starting_sea_elevation: float32 [256, 2048], P('lat', 'lon'), may hold values from -6 to 6
- zonal_integrated_flux: float32 [256, 2048], P('lat', 'lon'), may hold values from -6 to 6
- meridional_integrated_flux: float32 [256, 2048], P('lat', 'lon'), may hold values from -6 to 6
- ocean_strata_total: int32 [256, 2048], P('lat', 'lon'), may hold values from 0 to 8
- thermal_anomaly: float32 [8, 256, 2048], P(None, 'lat', 'lon'), may hold values from -6 to 6
- zonal_baroclinic_velocity: float32 [8, 256, 2048], P(None, 'lat', 'lon'), may hold values from -3 to 3
- meridional_baroclinic_velocity: float32 [8, 256, 2048], P(None, 'lat', 'lon'), may hold values from -3 to 3
- sent_sender_mesh_index: int32 [128, 128, 1024], P(('lat', 'lon')), may hold values from 0 to 4095
- sent_intersection_extent: float32 [128, 128, 1024], P(('lat', 'lon')), may hold values from 0.2 to 1
- sent_entry_tally: int32 [128, 128], P(('lat', 'lon')), may hold values from 0 to 1024, as said below
- received_atmosphere_mesh_index: int32 [128, 128, 1024], P(('lat', 'lon')), may hold values from 0 to 4095
Outputs:
- height_new: float32 [256, 2048], P('lat', 'lon')
- east_new: float32 [256, 2048], P('lat', 'lon')
- north_new: float32 [256, 2048], P('lat', 'lon')
- temperature_new: float32 [8, 256, 2048], P(None, 'lat', 'lon')
- atmosphere_fields: float32 [4, 524288], P(None, ('lat', 'lon'))
Inputs may be any that keep to these rules, and one draw needn't show every extreme that they name: Slots j >= sent_entry_tally[s, d] are unused. In every draw one owner receives exactly 1024 live slots from every device. `sent_sender_mesh_index`: A cell of the sending device's block, numbered row by row. `received_atmosphere_mesh_index`: an atmosphere cell of the receiving owner. `ocean_strata_total`: 0 is land.
All inputs are finite; a program needn't handle non-finite values.
Results may differ from a plain program's by a relative error of at most 0.00017.
Values sent between devices are 32-bit elements; how exact they have to be, the bound alone decides.
No kernel may reach another device: no remote copies, remote signals or barrier semaphores. Data moves between devices by JAX's collectives and lax.ppermute only.
A program may use at most 64 MiB of HBM per device.

v0:
```python
import math

import jax
import jax.numpy as jnp
from jax import lax
from jax.sharding import PartitionSpec as P

VERTICAL_STRATA = 8
STEPS = 4
NF = 4
ACELL = 4096


mass_coef = 0.7
slope_coef = 0.7
spin_coef = 0.3
mix_coef = 0.1
carry_coef = 0.1
block_limit = 8192


def with_halo(block, sides, width, periodic):
    for axis, dim in sides:
        count = lax.axis_size(axis)
        forward = [(i, i + 1) for i in range(count - 1)]
        if periodic:
            forward.append((count - 1, 0))
        backward = [(target, source) for source, target in forward]
        low = lax.ppermute(
            lax.slice_in_dim(block, block.shape[dim] - width, None, axis=dim), axis, forward
        )
        high = lax.ppermute(lax.slice_in_dim(block, 0, width, axis=dim), axis, backward)
        block = jnp.concatenate([low, block, high], axis=dim)
    return block


def widen(fields, signs, width):
    rows = fields.shape[1]
    lon_wide = with_halo(fields, (("lon", 2),), width, True)
    both_wide = with_halo(lon_wide, (("lat", 1),), width, False)
    upper = jnp.flip(lon_wide[:, rows - width :, :], axis=(1, 2))
    sectors = lax.axis_size("lon")
    collected = lax.all_gather(upper[None], "lon", axis=0, tiled=True)
    mirrored = lax.dynamic_index_in_dim(
        collected, sectors - 1 - lax.axis_index("lon"), 0, keepdims=False
    )
    folded = mirrored * signs[:, None, None]
    on_top = lax.axis_index("lat") == lax.axis_size("lat") - 1
    top_rim = jnp.where(on_top, folded, both_wide[:, rows + width :, :])
    return jnp.concatenate([both_wide[:, : rows + width, :], top_rim], axis=1)


def pick_cells(surface_grid, indices):
    fields_count, rows, columns = surface_grid.shape
    table = jnp.transpose(surface_grid, (2, 0, 1)).reshape(columns, fields_count * rows)
    total = indices.shape[0]
    size = math.gcd(total, block_limit)
    blocks = indices.reshape(total // size, size)
    column_ids = jnp.arange(columns)
    row_ids = jnp.arange(rows)

    def one_block(block):
        column_hot = (block[:, None] % columns == column_ids[None, :]).astype(jnp.float32)
        row_hot = (block[:, None] // columns == row_ids[None, :]).astype(jnp.float32)
        by_column = jnp.dot(
            column_hot, table, precision=lax.Precision.HIGHEST, preferred_element_type=jnp.float32
        )
        by_column = by_column.reshape(size, fields_count, rows)
        return jnp.sum(by_column * row_hot[:, None, :], axis=2)

    picked = lax.map(one_block, blocks).reshape(total, fields_count)
    return jnp.transpose(picked)


def spread_cells(values, targets, cells):
    fields_count = values.shape[0]
    total = targets.shape[0]
    size = math.gcd(total, block_limit)
    high_count = cells // 128
    value_blocks = jnp.transpose(values.reshape(fields_count, total // size, size), (1, 0, 2))
    target_blocks = targets.reshape(total // size, size)
    low_ids = jnp.arange(128)
    high_ids = jnp.arange(high_count)

    def add_block(carry, pieces):
        value_block, target_block = pieces
        low_hot = (target_block[:, None] % 128 == low_ids[None, :]).astype(jnp.float32)
        high_hot = (target_block[:, None] // 128 == high_ids[None, :]).astype(jnp.float32)
        weighted = (jnp.transpose(value_block)[:, :, None] * high_hot[:, None, :]).reshape(
            size, fields_count * high_count
        )
        term = lax.dot_general(
            weighted,
            low_hot,
            (((0,), (0,)), ((), ())),
            precision=lax.Precision.HIGHEST,
            preferred_element_type=jnp.float32,
        )
        return (carry + term, None)

    start = jnp.zeros((fields_count * high_count, 128), jnp.float32)
    summed, _ = lax.scan(add_block, start, (value_blocks, target_blocks))
    return summed.reshape(fields_count, cells)


def local(
    starting_sea_elevation,
    zonal_integrated_flux,
    meridional_integrated_flux,
    ocean_strata_total,
    thermal_anomaly,
    zonal_baroclinic_velocity,
    meridional_baroclinic_velocity,
    sent_sender_mesh_index,
    sent_intersection_extent,
    sent_entry_tally,
    received_atmosphere_mesh_index,
):
    band_rows = starting_sea_elevation.shape[0]
    grid_rows = band_rows * lax.axis_size("lat")
    band = lax.axis_index("lat")
    depth = ocean_strata_total.astype(jnp.float32)
    wet = (ocean_strata_total > 0).astype(jnp.float32)
    hnorm = depth / VERTICAL_STRATA
    height = starting_sea_elevation * wet
    east = zonal_integrated_flux * wet
    north = meridional_integrated_flux * wet
    rows = (band * band_rows + jnp.arange(band_rows)).astype(jnp.float32)
    rotation = (-spin_coef * jnp.cos(jnp.pi * (rows + 0.5) / grid_rows))[:, None]
    vector_signs = jnp.array([-1.0, -1.0], jnp.float32)
    scalar_signs = jnp.array([1.0], jnp.float32)
    for step in range(STEPS):
        moved = widen(jnp.stack([east, north]), vector_signs, 1)
        east_e = moved[0, 1:-1, 2:]
        east_w = moved[0, 1:-1, :-2]
        north_n = moved[1, 2:, 1:-1]
        north_s = moved[1, :-2, 1:-1]
        height = wet * (height - mass_coef * (east_e - east_w + (north_n - north_s)))
        height_wide = widen(height[None], scalar_signs, 1)[0]
        height_e = height_wide[1:-1, 2:]
        height_w = height_wide[1:-1, :-2]
        height_n = height_wide[2:, 1:-1]
        height_s = height_wide[:-2, 1:-1]
        east = wet * (east - slope_coef * hnorm * (height_e - height_w) + rotation * north)
        north = wet * (north - slope_coef * hnorm * (height_n - height_s) - rotation * east)
    levels_int = jnp.arange(VERTICAL_STRATA)[:, None, None]
    levels_float = jnp.arange(VERTICAL_STRATA).astype(jnp.float32)[:, None, None]
    submerged_stratum_mask = (levels_int < ocean_strata_total[None]).astype(jnp.float32)
    passive_scalar_values = thermal_anomaly * submerged_stratum_mask
    tracer_signs = jnp.ones((VERTICAL_STRATA + 1,), jnp.float32)
    widened = widen(jnp.concatenate([passive_scalar_values, depth[None]], axis=0), tracer_signs, 1)
    tracer_wide = widened[:VERTICAL_STRATA]
    wet_wide = (levels_float < widened[VERTICAL_STRATA][None]).astype(jnp.float32)
    tracer_e = tracer_wide[:, 1:-1, 2:]
    tracer_w = tracer_wide[:, 1:-1, :-2]
    tracer_n = tracer_wide[:, 2:, 1:-1]
    tracer_s = tracer_wide[:, :-2, 1:-1]
    wet_e = wet_wide[:, 1:-1, 2:]
    wet_w = wet_wide[:, 1:-1, :-2]
    wet_n = wet_wide[:, 2:, 1:-1]
    wet_s = wet_wide[:, :-2, 1:-1]
    mixing = (
        wet_e * (tracer_e - passive_scalar_values)
        + wet_w * (tracer_w - passive_scalar_values)
        + wet_n * (tracer_n - passive_scalar_values)
        + wet_s * (tracer_s - passive_scalar_values)
    )
    speed_east = east[None] + zonal_baroclinic_velocity
    speed_north = north[None] + meridional_baroclinic_velocity
    carried = speed_east * (tracer_e - tracer_w) + speed_north * (tracer_n - tracer_s)
    tracer_new = submerged_stratum_mask * (
        passive_scalar_values + mix_coef * mixing - carry_coef * carried
    )
    surface_grid = jnp.stack([height, speed_east[0], speed_north[0], tracer_new[0]])
    owners = sent_sender_mesh_index.shape[1]
    slots = sent_sender_mesh_index.shape[2]
    picked = pick_cells(surface_grid, sent_sender_mesh_index[0].reshape(-1)).reshape(
        NF, owners, slots
    )
    live = jnp.arange(slots)[None, :] < sent_entry_tally[0][:, None]
    values = jnp.where(live[None], sent_intersection_extent[0][None] * picked, 0.0)
    targets = received_atmosphere_mesh_index[0].reshape(-1)
    block = lax.all_to_all(values, ("lat", "lon"), split_axis=1, concat_axis=1, tiled=True)
    fields_count = block.shape[0]
    atmosphere = spread_cells(block.reshape(fields_count, -1), targets, ACELL)
    return (height, east, north, tracer_new, atmosphere)


def solution(mesh):
    in_specs = (
        P("lat", "lon"),
        P("lat", "lon"),
        P("lat", "lon"),
        P("lat", "lon"),
        P(None, "lat", "lon"),
        P(None, "lat", "lon"),
        P(None, "lat", "lon"),
        P(("lat", "lon"), None, None),
        P(("lat", "lon"), None, None),
        P(("lat", "lon"), None),
        P(("lat", "lon"), None, None),
    )
    out_specs = (
        P("lat", "lon"),
        P("lat", "lon"),
        P("lat", "lon"),
        P(None, "lat", "lon"),
        P(None, ("lat", "lon")),
    )
    return jax.shard_map(local, mesh=mesh, in_specs=in_specs, out_specs=out_specs, check_vma=False)
```

profile of v0, /device:TPU:1, one launch (start us, length us, event | category | flops | bytes accessed | tf_op | source)
XLA Modules:
  0.0 557.0 jit_solution(9308671634009213808)
XLA Ops:
  4.2 2.9 collective-permute-start.1
  14.3 3.5 collective-permute-start.3
  19.4 24.9 %all-gather = f32[32,1,130]{2,1,0:T(1,128)S(1)} all-gather(f32[2,1,130]{2,1,0:T(1,128)S(1)} %slice.507), channel_id=2, replica_groups=mesh['lat'=8,'lon'=16] {'lon'}, dimensions={0}, use_global_device_ids=true | all-gather | bytes 17680 | tf_op jit(solution)/shard_map/all_gather | solution.py:43
  44.5 2.9 collective-permute-start.4
  48.3 3.8 collective-permute-done.5
  52.1 4.3 collective-permute-start.6
  58.0 19.8 %all-gather.1 = f32[16,1,130]{2,1,0:T(1,128)S(1)} all-gather(f32[1,1,130]{2,1,0:T(1,128)S(1)} %slice.508), channel_id=3, replica_groups=mesh['lat'=8,'lon'=16] {'lon'}, dimensions={0}, use_global_device_ids=true | all-gather | bytes 8840 | tf_op jit(solution)/shard_map/all_gather | solution.py:43
  78.5 2.9 collective-permute-start.9
  81.4 4.2 collective-permute-start.34
  86.6 3.4 collective-permute-start.11
  91.5 20.9 %all-gather.2 = f32[32,1,130]{2,1,0:T(1,128)S(1)} all-gather(f32[2,1,130]{2,1,0:T(1,128)S(1)} %slice.509), channel_id=4, replica_groups=mesh['lat'=8,'lon'=16] {'lon'}, dimensions={0}, use_global_device_ids=true | all-gather | bytes 17680 | tf_op jit(solution)/shard_map/all_gather | solution.py:43
  112.7 3.3 collective-permute-start.12
  116.8 3.8 collective-permute-done.13
  120.7 4.3 collective-permute-start.14
  126.5 19.5 %all-gather.3 = f32[16,1,130]{2,1,0:T(1,128)S(1)} all-gather(f32[1,1,130]{2,1,0:T(1,128)S(1)} %slice.510), channel_id=5, replica_groups=mesh['lat'=8,'lon'=16] {'lon'}, dimensions={0}, use_global_device_ids=true | all-gather | bytes 8840 | tf_op jit(solution)/shard_map/all_gather | solution.py:43
  146.6 2.9 collective-permute-start.17
  149.6 19.8 %all-gather.8 = f32[144,1,130]{2,1,0:T(1,128)S(1)} all-gather(f32[9,1,130]{2,1,0:T(1,128)S(1)} %slice.515), channel_id=10, replica_groups=mesh['lat'=8,'lon'=16] {'lon'}, dimensions={0}, use_global_device_ids=true | all-gather | bytes 79560 | tf_op jit(solution)/shard_map/all_gather | solution.py:43
  169.5 6.1 %collective-permute-start.19 = (f32[2,1,130]{2,1,0:T(1,128)S(1)}, f32[2,1,130]{2,1,0:T(1,128)}, u32[]{:S(2)}, u32[]{:S(2)}) collective-permute-start(f32[2,1,130]{2,1,0:T(1,128)S(1)} %get-tuple-element.265), channel_id=1, source_target_pairs={{0,16},{16,32},{32,48},{48,64},{64,80},{80,96},{96,112},{1,17},{17... | collective-permute-start | bytes 3128 | tf_op jit(solution)/shard_map/ppermute | solution.py:29
  177.1 21.3 %all-gather.4 = f32[32,1,130]{2,1,0:T(1,128)S(1)} all-gather(f32[2,1,130]{2,1,0:T(1,128)S(1)} %slice.511), channel_id=6, replica_groups=mesh['lat'=8,'lon'=16] {'lon'}, dimensions={0}, use_global_device_ids=true | all-gather | bytes 17680 | tf_op jit(solution)/shard_map/all_gather | solution.py:43
  202.1 3.7 collective-permute-done.21
  205.8 4.3 collective-permute-start.22
  211.7 20.9 %all-gather.5 = f32[16,1,130]{2,1,0:T(1,128)S(1)} all-gather(f32[1,1,130]{2,1,0:T(1,128)S(1)} %slice.512), channel_id=7, replica_groups=mesh['lat'=8,'lon'=16] {'lon'}, dimensions={0}, use_global_device_ids=true | all-gather | bytes 8840 | tf_op jit(solution)/shard_map/all_gather | solution.py:43
  238.6 6.4 %collective-permute-start.27 = (f32[2,1,130]{2,1,0:T(1,128)S(1)}, f32[2,1,130]{2,1,0:T(1,128)S(1)}, u32[]{:S(2)}, u32[]{:S(2)}) collective-permute-start(f32[2,1,130]{2,1,0:T(1,128)S(1)} %get-tuple-element.263), channel_id=1, source_target_pairs={{0,16},{16,32},{32,48},{48,64},{64,80},{80,96},{96,112},{1,17},{17... | collective-permute-start | bytes 3128 | tf_op jit(solution)/shard_map/ppermute | solution.py:29
  246.5 24.1 %all-gather.6 = f32[32,1,130]{2,1,0:T(1,128)S(1)} all-gather(f32[2,1,130]{2,1,0:T(1,128)S(1)} %slice.513), channel_id=8, replica_groups=mesh['lat'=8,'lon'=16] {'lon'}, dimensions={0}, use_global_device_ids=true | all-gather | bytes 17680 | tf_op jit(solution)/shard_map/all_gather | solution.py:43
  270.8 3.3 collective-permute-start.28
  275.1 3.8 collective-permute-done.29
  280.1 7.1 %collective-permute-start.30 = (f32[1,1,130]{2,1,0:T(1,128)}, f32[1,1,130]{2,1,0:T(1,128)}, u32[]{:S(2)}, u32[]{:S(2)}) collective-permute-start(f32[1,1,130]{2,1,0:T(1,128)} %get-tuple-element.270), channel_id=1, source_target_pairs={{0,16},{16,32},{32,48},{48,64},{64,80},{80,96},{96,112},{1,17},{17... | collective-permute-start | bytes 1568 | tf_op jit(solution)/shard_map/ppermute | solution.py:29
  290.7 19.7 %all-gather.7 = f32[16,1,130]{2,1,0:T(1,128)S(1)} all-gather(f32[1,1,130]{2,1,0:T(1,128)S(1)} %slice.514), channel_id=9, replica_groups=mesh['lat'=8,'lon'=16] {'lon'}, dimensions={0}, use_global_device_ids=true | all-gather | bytes 8840 | tf_op jit(solution)/shard_map/all_gather | solution.py:43
  314.2 62.9 %while.26 = (s32[]{:T(128)}, f32[16,8192,4]{1,2,0:T(4,128)S(1)}, s32[16,8192]{1,0:T(8,128)S(1)}, f32[128,128]{1,0:T(8,128)S(1)}, s32[]{:T(128)}) while((s32[]{:T(128)}, f32[16,8192,4]{1,2,0:T(4,128)S(1)}, s32[16,8192]{1,0:T(8,128)S(1)}, f32[128,128]{1,0:T(8,128)S(1)}, s32[]{:T(128)}) %tuple.96), condition=%wide.region_2.3_spmd.clone, body=%wide.region_0.2_spmd.clone.sunk | while | flops 1614405632 | bytes 2785349 | solution.py:71
  314.3 3.7 multiply_reduce_fusion.2
  318.3 3.7 multiply_reduce_fusion.2
  322.2 3.7 multiply_reduce_fusion.2
  326.1 3.7 multiply_reduce_fusion.2
  330.1 3.7 multiply_reduce_fusion.2
  334.0 3.7 multiply_reduce_fusion.2
  337.9 3.7 multiply_reduce_fusion.2
  341.9 3.7 multiply_reduce_fusion.2
  345.8 3.7 multiply_reduce_fusion.2
  349.7 3.7 multiply_reduce_fusion.2
  353.7 3.7 multiply_reduce_fusion.2
  357.6 3.7 multiply_reduce_fusion.2
  361.5 3.7 multiply_reduce_fusion.2
  365.5 3.7 multiply_reduce_fusion.2
  369.4 3.7 multiply_reduce_fusion.2
  373.3 3.7 multiply_reduce_fusion.2
  382.2 14.8 %all-to-all-start = ((f32[4,128,1024]{2,0,1:T(4,128)}), f32[4,128,1024]{2,0,1:T(4,128)S(1)}, u32[]{:S(2)}, u32[]{:S(2)}) async-start(f32[4,128,1024]{2,0,1:T(4,128)} %copy.26), calls=%async_computation | async-start | bytes 4194304 | tf_op jit(solution)/shard_map/all_to_all | solution.py:183
  398.1 29.0 %all-to-all-done = f32[4,128,1024]{2,0,1:T(4,128)S(1)} async-done(((f32[4,128,1024]{2,0,1:T(4,128)}), f32[4,128,1024]{2,0,1:T(4,128)S(1)}, u32[]{:S(2)}, u32[]{:S(2)}) %all-to-all-start) | async-done | bytes 2097184 | tf_op jit(solution)/shard_map/all_to_all | solution.py:183
  431.5 124.9 %while.27 = (s32[]{:T(128)}, f32[128,128]{1,0:T(8,128)S(1)}, f32[16,4,8192]{2,0,1:T(8,128)S(1)}, s32[16,8192]{1,0:T(8,128)S(1)}, s32[]{:T(128)}, /*index=5*/s32[]{:T(128)}) while((s32[]{:T(128)}, f32[128,128]{1,0:T(8,128)S(1)}, f32[16,4,8192]{2,0,1:T(8,128)S(1)}, s32[16,8192]{1,0:T(8,128)S(1)}, s32[]{:T(128)}, ...), condition=%wide.region_4.5_spmd.clone, body=%wide.region_3.4_spmd.clone.sunk | while | flops 1613422592 | bytes 11501655 | solution.py:102
  434.3 5.0 fusion.118
  442.1 5.0 fusion.118
  449.9 5.0 fusion.118
  457.7 5.0 fusion.118
  465.5 5.0 fusion.118
  473.3 5.0 fusion.118
  481.1 5.0 fusion.118
  488.9 5.0 fusion.118
  496.7 5.0 fusion.118
  504.5 5.0 fusion.118
  512.3 5.0 fusion.118
  520.1 5.0 fusion.118
  528.0 5.0 fusion.118
  535.8 5.0 fusion.118
  543.6 5.0 fusion.118
  551.4 5.0 fusion.118
  (326 shorter events, 103.3 us)
Async XLA Ops:
  0.6 77.3 %copy-start.10 = (f32[32,128]{1,0:T(8,128)S(1)}, f32[32,128]{1,0:T(8,128)}, u32[]{:S(2)}) copy-start(f32[32,128]{1,0:T(8,128)} %param.18) | copy-start | bytes 49156
  0.6 77.3 %copy-start = (s32[32,128]{1,0:T(8,128)S(1)}, s32[32,128]{1,0:T(8,128)}, u32[]{:S(2)}) copy-start(s32[32,128]{1,0:T(8,128)} %param.20) | copy-start | bytes 49156
  0.7 77.3 %copy-start.11 = (f32[32,128]{1,0:T(8,128)S(1)}, f32[32,128]{1,0:T(8,128)}, u32[]{:S(2)}) copy-start(f32[32,128]{1,0:T(8,128)} %param.19) | copy-start | bytes 49156
  0.7 43.6 %copy-start.14 = (f32[32,128]{1,0:T(8,128)S(1)}, f32[32,128]{1,0:T(8,128)}, u32[]{:S(2)}) copy-start(f32[32,128]{1,0:T(8,128)} %param.17) | copy-start | bytes 49156
  1.4 269.2 %copy-start.5 = (pred[32,128]{1,0:T(8,128)(4,1)}, pred[32,128]{1,0:T(8,128)(4,1)S(1)}, u32[]{:S(2)}) copy-start(pred[32,128]{1,0:T(8,128)(4,1)S(1)} %get-tuple-element.253) | copy-start | bytes 12292
  2.9 11.3 %collective-permute-start = (f32[2,32,1]{2,1,0:T(8,128)}, f32[2,32,1]{2,1,0:T(8,128)S(1)}, u32[]{:S(2)}, u32[]{:S(2)}) collective-permute-start(f32[2,32,1]{2,1,0:T(8,128)} %get-tuple-element.285), channel_id=1, source_target_pairs={{1,0},{2,1},{3,2},{4,3},{5,4},{6,5},{7,6},{8,7},{9,8},{10,9},{11,1... | collective-permute-start | bytes 776 | tf_op jit(solution)/shard_map/ppermute | solution.py:32
  4.2 9.9 %collective-permute-start.1 = (f32[2,32,1]{2,1,0:T(8,128)}, f32[2,32,1]{2,1,0:T(8,128)S(1)}, u32[]{:S(2)}, u32[]{:S(2)}) collective-permute-start(f32[2,32,1]{2,1,0:T(8,128)} %get-tuple-element.284), channel_id=1, source_target_pairs={{0,1},{1,2},{2,3},{3,4},{4,5},{5,6},{6,7},{7,8},{8,9},{9,10},{10,1... | collective-permute-start | bytes 776 | tf_op jit(solution)/shard_map/ppermute | solution.py:29
  7.9 229.0 %copy-start.2 = (f32[1,32,128]{2,1,0:T(8,128)}, f32[1,32,128]{2,1,0:T(8,128)S(1)}, u32[]{:S(2)}) copy-start(f32[1,32,128]{2,1,0:T(8,128)S(1)} %convert_bitcast_fusion) | copy-start | bytes 49156
  9.6 37.8 %collective-permute-start.32 = (f32[9,32,1]{2,1,0:T(8,128)}, f32[9,32,1]{2,1,0:T(8,128)S(1)}, u32[]{:S(2)}, u32[]{:S(2)}) collective-permute-start(f32[9,32,1]{2,1,0:T(8,128)} %get-tuple-element.260), channel_id=1, source_target_pairs={{0,1},{1,2},{2,3},{3,4},{4,5},{5,6},{6,7},{7,8},{8,9},{9,10},{10,1... | collective-permute-start | bytes 3464 | tf_op jit(solution)/shard_map/ppermute | solution.py:29
  10.1 37.3 %collective-permute-start.33 = (f32[9,32,1]{2,1,0:T(8,128)S(1)}, f32[9,32,1]{2,1,0:T(8,128)S(1)}, u32[]{:S(2)}, u32[]{:S(2)}) collective-permute-start(f32[9,32,1]{2,1,0:T(8,128)S(1)} %get-tuple-element.261), channel_id=1, source_target_pairs={{1,0},{2,1},{3,2},{4,3},{5,4},{6,5},{7,6},{8,7},{9,8},{10,9},{11,1... | collective-permute-start | bytes 3464 | tf_op jit(solution)/shard_map/ppermute | solution.py:32
  12.2 187.0 %copy-start.15 = (f32[32]{0:T(128)}, f32[32]{0:T(128)S(1)}, u32[]{:S(2)}) copy-start(f32[32]{0:T(128)S(1)} %cosine_multiply_fusion) | copy-start | bytes 388
  14.3 30.0 %collective-permute-start.3 = (f32[2,1,130]{2,1,0:T(1,128)S(1)}, f32[2,1,130]{2,1,0:T(1,128)S(1)}, u32[]{:S(2)}, u32[]{:S(2)}) collective-permute-start(f32[2,1,130]{2,1,0:T(1,128)S(1)} %get-tuple-element.269), channel_id=1, source_target_pairs={{0,16},{16,32},{32,48},{48,64},{64,80},{80,96},{96,112},{1,17},{17... | collective-permute-start | bytes 3128 | tf_op jit(solution)/shard_map/ppermute | solution.py:29
  18.1 26.2 %collective-permute-start.2 = (f32[2,1,130]{2,1,0:T(1,128)S(1)}, f32[2,1,130]{2,1,0:T(1,128)S(1)}, u32[]{:S(2)}, u32[]{:S(2)}) collective-permute-start(f32[2,1,130]{2,1,0:T(1,128)S(1)} %get-tuple-element.268), channel_id=1, source_target_pairs={{16,0},{32,16},{48,32},{64,48},{80,64},{96,80},{112,96},{17,1},{33... | collective-permute-start | bytes 3128 | tf_op jit(solution)/shard_map/ppermute | solution.py:32
  44.5 3.8 collective-permute-start.4
  47.4 4.7 collective-permute-start.5
  52.1 25.7 %collective-permute-start.6 = (f32[1,1,130]{2,1,0:T(1,128)S(1)}, f32[1,1,130]{2,1,0:T(1,128)S(1)}, u32[]{:S(2)}, u32[]{:S(2)}) collective-permute-start(f32[1,1,130]{2,1,0:T(1,128)S(1)} %get-tuple-element.276), channel_id=1, source_target_pairs={{0,16},{16,32},{32,48},{48,64},{64,80},{80,96},{96,112},{1,17},{17... | collective-permute-start | bytes 1568 | tf_op jit(solution)/shard_map/ppermute | solution.py:29
  56.7 21.1 %collective-permute-start.7 = (f32[1,1,130]{2,1,0:T(1,128)S(1)}, f32[1,1,130]{2,1,0:T(1,128)S(1)}, u32[]{:S(2)}, u32[]{:S(2)}) collective-permute-start(f32[1,1,130]{2,1,0:T(1,128)S(1)} %get-tuple-element.277), channel_id=1, source_target_pairs={{16,0},{32,16},{48,32},{64,48},{80,64},{96,80},{112,96},{17,1},{33... | collective-permute-start | bytes 1568 | tf_op jit(solution)/shard_map/ppermute | solution.py:32
  78.1 8.4 %collective-permute-start.8 = (f32[2,32,1]{2,1,0:T(8,128)S(1)}, f32[2,32,1]{2,1,0:T(8,128)S(1)}, u32[]{:S(2)}, u32[]{:S(2)}) collective-permute-start(f32[2,32,1]{2,1,0:T(8,128)S(1)} %get-tuple-element.283), channel_id=1, source_target_pairs={{1,0},{2,1},{3,2},{4,3},{5,4},{6,5},{7,6},{8,7},{9,8},{10,9},{11,1... | collective-permute-start | bytes 776 | tf_op jit(solution)/shard_map/ppermute | solution.py:32
  78.5 8.0 %collective-permute-start.9 = (f32[2,32,1]{2,1,0:T(8,128)S(1)}, f32[2,32,1]{2,1,0:T(8,128)S(1)}, u32[]{:S(2)}, u32[]{:S(2)}) collective-permute-start(f32[2,32,1]{2,1,0:T(8,128)S(1)} %get-tuple-element.282), channel_id=1, source_target_pairs={{0,1},{1,2},{2,3},{3,4},{4,5},{5,6},{6,7},{7,8},{8,9},{9,10},{10,1... | collective-permute-start | bytes 776 | tf_op jit(solution)/shard_map/ppermute | solution.py:29
  81.4 155.5 %collective-permute-start.34 = (f32[9,1,130]{2,1,0:T(1,128)}, f32[9,1,130]{2,1,0:T(1,128)S(1)}, u32[]{:S(2)}, u32[]{:S(2)}) collective-permute-start(f32[9,1,130]{2,1,0:T(1,128)} %get-tuple-element.258), channel_id=1, source_target_pairs={{0,16},{16,32},{32,48},{48,64},{64,80},{80,96},{96,112},{1,17},{17... | collective-permute-start | bytes 14048 | tf_op jit(solution)/shard_map/ppermute | solution.py:29
  86.6 25.9 %collective-permute-start.11 = (f32[2,1,130]{2,1,0:T(1,128)S(1)}, f32[2,1,130]{2,1,0:T(1,128)S(1)}, u32[]{:S(2)}, u32[]{:S(2)}) collective-permute-start(f32[2,1,130]{2,1,0:T(1,128)S(1)} %get-tuple-element.267), channel_id=1, source_target_pairs={{0,16},{16,32},{32,48},{48,64},{64,80},{80,96},{96,112},{1,17},{17... | collective-permute-start | bytes 3128 | tf_op jit(solution)/shard_map/ppermute | solution.py:29
  90.3 22.2 %collective-permute-start.10 = (f32[2,1,130]{2,1,0:T(1,128)S(1)}, f32[2,1,130]{2,1,0:T(1,128)S(1)}, u32[]{:S(2)}, u32[]{:S(2)}) collective-permute-start(f32[2,1,130]{2,1,0:T(1,128)S(1)} %get-tuple-element.266), channel_id=1, source_target_pairs={{16,0},{32,16},{48,32},{64,48},{80,64},{96,80},{112,96},{17,1},{33... | collective-permute-start | bytes 3128 | tf_op jit(solution)/shard_map/ppermute | solution.py:32
  112.7 4.1 collective-permute-start.12
  115.9 4.7 collective-permute-start.13
  120.7 25.3 %collective-permute-start.14 = (f32[1,1,130]{2,1,0:T(1,128)S(1)}, f32[1,1,130]{2,1,0:T(1,128)S(1)}, u32[]{:S(2)}, u32[]{:S(2)}) collective-permute-start(f32[1,1,130]{2,1,0:T(1,128)S(1)} %get-tuple-element.274), channel_id=1, source_target_pairs={{0,16},{16,32},{32,48},{48,64},{64,80},{80,96},{96,112},{1,17},{17... | collective-permute-start | bytes 1568 | tf_op jit(solution)/shard_map/ppermute | solution.py:29
  125.2 20.8 %collective-permute-start.15 = (f32[1,1,130]{2,1,0:T(1,128)S(1)}, f32[1,1,130]{2,1,0:T(1,128)S(1)}, u32[]{:S(2)}, u32[]{:S(2)}) collective-permute-start(f32[1,1,130]{2,1,0:T(1,128)S(1)} %get-tuple-element.275), channel_id=1, source_target_pairs={{16,0},{32,16},{48,32},{64,48},{80,64},{96,80},{112,96},{17,1},{33... | collective-permute-start | bytes 1568 | tf_op jit(solution)/shard_map/ppermute | solution.py:32
  146.3 23.1 %collective-permute-start.16 = (f32[2,32,1]{2,1,0:T(8,128)S(1)}, f32[2,32,1]{2,1,0:T(8,128)S(1)}, u32[]{:S(2)}, u32[]{:S(2)}) collective-permute-start(f32[2,32,1]{2,1,0:T(8,128)S(1)} %get-tuple-element.281), channel_id=1, source_target_pairs={{1,0},{2,1},{3,2},{4,3},{5,4},{6,5},{7,6},{8,7},{9,8},{10,9},{11,1... | collective-permute-start | bytes 776 | tf_op jit(solution)/shard_map/ppermute | solution.py:32
  146.6 22.7 %collective-permute-start.17 = (f32[2,32,1]{2,1,0:T(8,128)S(1)}, f32[2,32,1]{2,1,0:T(8,128)S(1)}, u32[]{:S(2)}, u32[]{:S(2)}) collective-permute-start(f32[2,32,1]{2,1,0:T(8,128)S(1)} %get-tuple-element.280), channel_id=1, source_target_pairs={{0,1},{1,2},{2,3},{3,4},{4,5},{5,6},{6,7},{7,8},{8,9},{9,10},{10,1... | collective-permute-start | bytes 776 | tf_op jit(solution)/shard_map/ppermute | solution.py:29
  169.5 29.0 %collective-permute-start.19 = (f32[2,1,130]{2,1,0:T(1,128)S(1)}, f32[2,1,130]{2,1,0:T(1,128)}, u32[]{:S(2)}, u32[]{:S(2)}) collective-permute-start(f32[2,1,130]{2,1,0:T(1,128)S(1)} %get-tuple-element.265), channel_id=1, source_target_pairs={{0,16},{16,32},{32,48},{48,64},{64,80},{80,96},{96,112},{1,17},{17... | collective-permute-start | bytes 3128 | tf_op jit(solution)/shard_map/ppermute | solution.py:29
  175.8 22.6 %collective-permute-start.18 = (f32[2,1,130]{2,1,0:T(1,128)S(1)}, f32[2,1,130]{2,1,0:T(1,128)S(1)}, u32[]{:S(2)}, u32[]{:S(2)}) collective-permute-start(f32[2,1,130]{2,1,0:T(1,128)S(1)} %get-tuple-element.264), channel_id=1, source_target_pairs={{16,0},{32,16},{48,32},{64,48},{80,64},{96,80},{112,96},{17,1},{33... | collective-permute-start | bytes 3128 | tf_op jit(solution)/shard_map/ppermute | solution.py:32
  199.3 2.8 collective-permute-start.20
  200.8 5.0 collective-permute-start.21
  200.8 31.8 %collective-permute-start.35 = (f32[9,1,130]{2,1,0:T(1,128)}, f32[9,1,130]{2,1,0:T(1,128)S(1)}, u32[]{:S(2)}, u32[]{:S(2)}) collective-permute-start(f32[9,1,130]{2,1,0:T(1,128)} %get-tuple-element.259), channel_id=1, source_target_pairs={{16,0},{32,16},{48,32},{64,48},{80,64},{96,80},{112,96},{17,1},{33... | collective-permute-start | bytes 14048 | tf_op jit(solution)/shard_map/ppermute | solution.py:32
  205.8 26.8 %collective-permute-start.22 = (f32[1,1,130]{2,1,0:T(1,128)S(1)}, f32[1,1,130]{2,1,0:T(1,128)S(1)}, u32[]{:S(2)}, u32[]{:S(2)}) collective-permute-start(f32[1,1,130]{2,1,0:T(1,128)S(1)} %get-tuple-element.272), channel_id=1, source_target_pairs={{0,16},{16,32},{32,48},{48,64},{64,80},{80,96},{96,112},{1,17},{17... | collective-permute-start | bytes 1568 | tf_op jit(solution)/shard_map/ppermute | solution.py:29
  210.4 22.3 %collective-permute-start.23 = (f32[1,1,130]{2,1,0:T(1,128)S(1)}, f32[1,1,130]{2,1,0:T(1,128)S(1)}, u32[]{:S(2)}, u32[]{:S(2)}) collective-permute-start(f32[1,1,130]{2,1,0:T(1,128)S(1)} %get-tuple-element.273), channel_id=1, source_target_pairs={{16,0},{32,16},{48,32},{64,48},{80,64},{96,80},{112,96},{17,1},{33... | collective-permute-start | bytes 1568 | tf_op jit(solution)/shard_map/ppermute | solution.py:32
  232.6 38.0 %copy-start.7 = (f32[9,1,130]{2,1,0:T(1,128)}, f32[9,1,130]{2,1,0:T(1,128)S(1)}, u32[]{:S(2)}) copy-start(f32[9,1,130]{2,1,0:T(1,128)S(1)} %broadcast_select_fusion) | copy-start | bytes 14044
  233.5 40.6 %copy-start.3 = (f32[32,128]{1,0:T(8,128)}, f32[32,128]{1,0:T(8,128)S(1)}, u32[]{:S(2)}) copy-start(f32[32,128]{1,0:T(8,128)S(1)} %get-tuple-element.246) | copy-start | bytes 49156
  233.5 40.6 %copy-start.4 = (f32[32,128]{1,0:T(8,128)}, f32[32,128]{1,0:T(8,128)S(1)}, u32[]{:S(2)}) copy-start(f32[32,128]{1,0:T(8,128)S(1)} %get-tuple-element.247) | copy-start | bytes 49156
  233.6 4.9 collective-permute-start.24
  234.0 4.5 collective-permute-start.25
  236.9 37.2 %copy-start.13 = (f32[9,1,130]{2,1,0:T(1,128)}, f32[9,1,130]{2,1,0:T(1,128)S(1)}, u32[]{:S(2)}) copy-start(f32[9,1,130]{2,1,0:T(1,128)S(1)} %collective-permute-done.34) | copy-start | bytes 14044
  238.6 32.1 %collective-permute-start.27 = (f32[2,1,130]{2,1,0:T(1,128)S(1)}, f32[2,1,130]{2,1,0:T(1,128)S(1)}, u32[]{:S(2)}, u32[]{:S(2)}) collective-permute-start(f32[2,1,130]{2,1,0:T(1,128)S(1)} %get-tuple-element.263), channel_id=1, source_target_pairs={{0,16},{16,32},{32,48},{48,64},{64,80},{80,96},{96,112},{1,17},{17... | collective-permute-start | bytes 3128 | tf_op jit(solution)/shard_map/ppermute | solution.py:29
  245.2 25.4 %collective-permute-start.26 = (f32[2,1,130]{2,1,0:T(1,128)S(1)}, f32[2,1,130]{2,1,0:T(1,128)S(1)}, u32[]{:S(2)}, u32[]{:S(2)}) collective-permute-start(f32[2,1,130]{2,1,0:T(1,128)S(1)} %get-tuple-element.262), channel_id=1, source_target_pairs={{16,0},{32,16},{48,32},{64,48},{80,64},{96,80},{112,96},{17,1},{33... | collective-permute-start | bytes 3128 | tf_op jit(solution)/shard_map/ppermute | solution.py:32
  270.7 43.4 %copy-start.1 = (f32[32,128]{1,0:T(8,128)}, f32[32,128]{1,0:T(8,128)S(1)}, u32[]{:S(2)}) copy-start(f32[32,128]{1,0:T(8,128)S(1)} %fusion.42) | copy-start | bytes 49156
  270.8 4.2 collective-permute-start.28
  274.1 4.7 collective-permute-start.29
  278.8 0.6 copy-start.12
  280.1 30.2 %collective-permute-start.30 = (f32[1,1,130]{2,1,0:T(1,128)}, f32[1,1,130]{2,1,0:T(1,128)}, u32[]{:S(2)}, u32[]{:S(2)}) collective-permute-start(f32[1,1,130]{2,1,0:T(1,128)} %get-tuple-element.270), channel_id=1, source_target_pairs={{0,16},{16,32},{32,48},{48,64},{64,80},{80,96},{96,112},{1,17},{17... | collective-permute-start | bytes 1568 | tf_op jit(solution)/shard_map/ppermute | solution.py:29
  289.4 21.0 %collective-permute-start.31 = (f32[1,1,130]{2,1,0:T(1,128)}, f32[1,1,130]{2,1,0:T(1,128)S(1)}, u32[]{:S(2)}, u32[]{:S(2)}) collective-permute-start(f32[1,1,130]{2,1,0:T(1,128)} %get-tuple-element.271), channel_id=1, source_target_pairs={{16,0},{32,16},{48,32},{64,48},{80,64},{96,80},{112,96},{17,1},{33... | collective-permute-start | bytes 1568 | tf_op jit(solution)/shard_map/ppermute | solution.py:32
  312.0 1.5 copy-start.9
  312.0 2.2 copy-start.8
  313.4 0.7 copy-start.6
  382.2 45.0 %all-to-all-start = ((f32[4,128,1024]{2,0,1:T(4,128)}), f32[4,128,1024]{2,0,1:T(4,128)S(1)}, u32[]{:S(2)}, u32[]{:S(2)}) async-start(f32[4,128,1024]{2,0,1:T(4,128)} %copy.26), calls=%async_computation | async-start | bytes 4194304 | tf_op jit(solution)/shard_map/all_to_all | solution.py:183
where the time goes:
time: 559 us; the launch traced here: 557 us
  blocking collectives  191 us (34%)
  matrix products  139 us (25%)
  starting transfers between devices  97 us (17%)
  other arithmetic  59.9 us (11%)
  waiting for transfers between devices  45.9 us (8%)
  local copies, waits for them, and re-layouts  21.1 us (4%)
    all_gather x9, blocking collectives, widen(): collected = lax.all_gather(upper[None], 'lon', axis=0, tiled=True)  191 us
    dot_general x16, matrix products, add_block(): lax.dot_general(weighted, low_hot, (((0,), (0,)), ((), ())), precision=la...  79.6 us
    ppermute x18, starting transfers between devices, with_halo(): lax.ppermute(lax.slice_in_dim(block, block.shape[dim] - width, None, axis...  66.6 us
    dot_general x16, matrix products, one_block(): jnp.dot(column_hot, table, precision=lax.Precision.HIGHEST, preferred_ele...  59.5 us
    mul x16, other arithmetic, add_block(): jnp.transpose(value_block)[:, :, None] * high_hot[:, None, :]  39.1 us
    all_to_all x1, waiting for transfers between devices, local(): lax.all_to_all(values, ('lat', 'lon'), split_axis=1, concat_axis=1, tiled...  29 us
    ppermute x18, waiting for transfers between devices, with_halo(): lax.ppermute(lax.slice_in_dim(block, 0, width, axis=dim), axis, backward)  15.9 us
    ppermute x18, starting transfers between devices, with_halo(): lax.ppermute(lax.slice_in_dim(block, 0, width, axis=dim), axis, backward)  15.6 us
  transfers between devices with their start and end apart: 37, of which 8 were waited for; matrix products, arithmetic and copies ran while one was open for 3% of the time, Pallas kernels for 0%

commit v1 on v0

--- a/solution.py
+++ b/solution.py
@@ -19,35 +19,46 @@
 block_limit = 8192
 
 
-def with_halo(block, sides, width, periodic):
-    for axis, dim in sides:
-        count = lax.axis_size(axis)
-        forward = [(i, i + 1) for i in range(count - 1)]
-        if periodic:
-            forward.append((count - 1, 0))
-        backward = [(target, source) for source, target in forward]
-        low = lax.ppermute(
-            lax.slice_in_dim(block, block.shape[dim] - width, None, axis=dim), axis, forward
-        )
-        high = lax.ppermute(lax.slice_in_dim(block, 0, width, axis=dim), axis, backward)
-        block = jnp.concatenate([low, block, high], axis=dim)
-    return block
-
-
-def widen(fields, signs, width):
-    rows = fields.shape[1]
-    lon_wide = with_halo(fields, (("lon", 2),), width, True)
-    both_wide = with_halo(lon_wide, (("lat", 1),), width, False)
-    upper = jnp.flip(lon_wide[:, rows - width :, :], axis=(1, 2))
+HALO = 2 * STEPS
+
+
+def exchange(block, signs, width):
+    planes, rows, columns = block.shape
     sectors = lax.axis_size("lon")
-    collected = lax.all_gather(upper[None], "lon", axis=0, tiled=True)
-    mirrored = lax.dynamic_index_in_dim(
-        collected, sectors - 1 - lax.axis_index("lon"), 0, keepdims=False
-    )
-    folded = mirrored * signs[:, None, None]
-    on_top = lax.axis_index("lat") == lax.axis_size("lat") - 1
-    top_rim = jnp.where(on_top, folded, both_wide[:, rows + width :, :])
-    return jnp.concatenate([both_wide[:, : rows + width, :], top_rim], axis=1)
+    bands = lax.axis_size("lat")
+    eastward = [(i, (i + 1) % sectors) for i in range(sectors)]
+    westward = [((i + 1) % sectors, i) for i in range(sectors)]
+    from_west = lax.ppermute(block[:, :, columns - width :], "lon", eastward)
+    from_east = lax.ppermute(block[:, :, :width], "lon", westward)
+    wide = jnp.concatenate([from_west, block, from_east], axis=2)
+    upward = [(b, b + 1) for b in range(bands - 1)]
+    downward = [(b + 1, b) for b in range(bands - 1)]
+    top = wide[:, rows - width :, :]
+    from_south = lax.ppermute(top, "lat", upward)
+    from_north = lax.ppermute(wide[:, :width, :], "lat", downward)
+    last = (bands - 1) * sectors
+    mirror = [(last + j, last + sectors - 1 - j) for j in range(sectors)]
+    folded = lax.ppermute(top, ("lat", "lon"), mirror)
+    folded = jnp.flip(folded, axis=(1, 2)) * signs[:, None, None]
+    on_top = lax.axis_index("lat") == bands - 1
+    north_rim = jnp.where(on_top, folded, from_north)
+    return jnp.concatenate([from_south, wide, north_rim], axis=1)
+
+
+def east_of(x):
+    return jnp.concatenate([x[..., 1:], x[..., -1:]], axis=-1)
+
+
+def west_of(x):
+    return jnp.concatenate([x[..., :1], x[..., :-1]], axis=-1)
+
+
+def north_of(x):
+    return jnp.concatenate([x[..., 1:, :], x[..., -1:, :]], axis=-2)
+
+
+def south_of(x):
+    return jnp.concatenate([x[..., :1, :], x[..., :-1, :]], axis=-2)
 
 
 def pick_cells(surface_grid, indices):
@@ -116,49 +127,52 @@
     sent_entry_tally,
     received_atmosphere_mesh_index,
 ):
-    band_rows = starting_sea_elevation.shape[0]
+    band_rows, band_columns = starting_sea_elevation.shape
     grid_rows = band_rows * lax.axis_size("lat")
     band = lax.axis_index("lat")
     depth = ocean_strata_total.astype(jnp.float32)
-    wet = (ocean_strata_total > 0).astype(jnp.float32)
-    hnorm = depth / VERTICAL_STRATA
-    height = starting_sea_elevation * wet
-    east = zonal_integrated_flux * wet
-    north = meridional_integrated_flux * wet
-    rows = (band * band_rows + jnp.arange(band_rows)).astype(jnp.float32)
+    planes = jnp.concatenate(
+        [
+            jnp.stack([starting_sea_elevation, zonal_integrated_flux, meridional_integrated_flux, depth]),
+            thermal_anomaly,
+        ],
+        axis=0,
+    )
+    signs = jnp.array([1.0, -1.0, -1.0] + [1.0] * (1 + VERTICAL_STRATA), jnp.float32)
+    ext = exchange(planes, signs, HALO)
+    depth_ext = ext[3]
+    wet = (depth_ext > 0).astype(jnp.float32)
+    hnorm = depth_ext / VERTICAL_STRATA
+    height = ext[0] * wet
+    east = ext[1] * wet
+    north = ext[2] * wet
+    global_rows = band * band_rows - HALO + jnp.arange(band_rows + 2 * HALO)
+    global_rows = jnp.where(global_rows >= grid_rows, 2 * grid_rows - 1 - global_rows, global_rows)
+    rows = global_rows.astype(jnp.float32)
     rotation = (-spin_coef * jnp.cos(jnp.pi * (rows + 0.5) / grid_rows))[:, None]
-    vector_signs = jnp.array([-1.0, -1.0], jnp.float32)
-    scalar_signs = jnp.array([1.0], jnp.float32)
     for step in range(STEPS):
-        moved = widen(jnp.stack([east, north]), vector_signs, 1)
-        east_e = moved[0, 1:-1, 2:]
-        east_w = moved[0, 1:-1, :-2]
-        north_n = moved[1, 2:, 1:-1]
-        north_s = moved[1, :-2, 1:-1]
-        height = wet * (height - mass_coef * (east_e - east_w + (north_n - north_s)))
-        height_wide = widen(height[None], scalar_signs, 1)[0]
-        height_e = height_wide[1:-1, 2:]
-        height_w = height_wide[1:-1, :-2]
-        height_n = height_wide[2:, 1:-1]
-        height_s = height_wide[:-2, 1:-1]
-        east = wet * (east - slope_coef * hnorm * (height_e - height_w) + rotation * north)
-        north = wet * (north - slope_coef * hnorm * (height_n - height_s) - rotation * east)
-    levels_int = jnp.arange(VERTICAL_STRATA)[:, None, None]
+        height = wet * (height - mass_coef * (east_of(east) - west_of(east) + (north_of(north) - south_of(north))))
+        east = wet * (east - slope_coef * hnorm * (east_of(height) - west_of(height)) + rotation * north)
+        north = wet * (north - slope_coef * hnorm * (north_of(height) - south_of(height)) - rotation * east)
+    inner = (slice(HALO, HALO + band_rows), slice(HALO, HALO + band_columns))
+    height = height[inner]
+    east = east[inner]
+    north = north[inner]
+    near = (slice(None), slice(HALO - 1, HALO + band_rows + 1), slice(HALO - 1, HALO + band_columns + 1))
     levels_float = jnp.arange(VERTICAL_STRATA).astype(jnp.float32)[:, None, None]
-    submerged_stratum_mask = (levels_int < ocean_strata_total[None]).astype(jnp.float32)
-    passive_scalar_values = thermal_anomaly * submerged_stratum_mask
-    tracer_signs = jnp.ones((VERTICAL_STRATA + 1,), jnp.float32)
-    widened = widen(jnp.concatenate([passive_scalar_values, depth[None]], axis=0), tracer_signs, 1)
-    tracer_wide = widened[:VERTICAL_STRATA]
-    wet_wide = (levels_float < widened[VERTICAL_STRATA][None]).astype(jnp.float32)
-    tracer_e = tracer_wide[:, 1:-1, 2:]
-    tracer_w = tracer_wide[:, 1:-1, :-2]
-    tracer_n = tracer_wide[:, 2:, 1:-1]
-    tracer_s = tracer_wide[:, :-2, 1:-1]
-    wet_e = wet_wide[:, 1:-1, 2:]
-    wet_w = wet_wide[:, 1:-1, :-2]
-    wet_n = wet_wide[:, 2:, 1:-1]
-    wet_s = wet_wide[:, :-2, 1:-1]
+    wet_wide = (levels_float < depth_ext[None][near]).astype(jnp.float32)
+    tracer_wide = ext[4:][near] * wet_wide
+    centre = (slice(None), slice(1, -1), slice(1, -1))
+    submerged_stratum_mask = wet_wide[centre]
+    passive_scalar_values = tracer_wide[centre]
+    tracer_e = east_of(tracer_wide)[centre]
+    tracer_w = west_of(tracer_wide)[centre]
+    tracer_n = north_of(tracer_wide)[centre]
+    tracer_s = south_of(tracer_wide)[centre]
+    wet_e = east_of(wet_wide)[centre]
+    wet_w = west_of(wet_wide)[centre]
+    wet_n = north_of(wet_wide)[centre]
+    wet_s = south_of(wet_wide)[centre]
     mixing = (
         wet_e * (tracer_e - passive_scalar_values)
         + wet_w * (tracer_w - passive_scalar_values)

time: 559 us -> 207 us (0.37)
  blocking collectives: 191 us -> 0 us
  starting transfers between devices: 97 us -> 24.7 us
  other arithmetic: 59.9 us -> 17.7 us
  matrix products: 139 us -> 104 us
  waiting for transfers between devices: 45.9 us -> 35.8 us
    all_gather x9 -> x0, blocking collectives: 191 us -> none  [widen(): collected = lax.all_gather(upper[None], 'lon', axis=0, tiled=True)]
    ppermute x36 -> x5, starting transfers between devices: 82.2 us -> 11.3 us  [the longest x1 4.36 us: exchange(): from_west = lax.ppermute(block[:, :, columns - width:], 'lon', eastward)]
    dot_general x16, matrix products: 79.6 us -> 44.7 us  [add_block(): lax.dot_general(weighted, low_hot, (((0,), (0,)), ((), ())), precision=la...]
    mul x16, other arithmetic: 39.1 us -> 6.53 us  [add_block(): jnp.transpose(value_block)[:, :, None] * high_hot[:, None, :]]
    ppermute x36 -> x5, waiting for transfers between devices: 16.9 us -> 6.4 us  [the longest x1 4.6 us: exchange(): from_east = lax.ppermute(block[:, :, :width], 'lon', westward)]
  transfers between devices with their start and end apart: 37 -> 6, of which waited for: 8 -> 3; matrix products, arithmetic and copies ran while one was open for 3% -> 3% of each run, Pallas kernels for 0% -> 0%
where the time goes in v1:
time: 207 us; the launch traced here: 206 us
  matrix products  104 us (50%)
  waiting for transfers between devices  35.8 us (17%)
  starting transfers between devices  24.7 us (12%)
  local copies, waits for them, and re-layouts  20.9 us (10%)
  other arithmetic  17.7 us (9%)
    dot_general x16, matrix products, one_block(): jnp.dot(column_hot, table, precision=lax.Precision.HIGHEST, preferred_ele...  59.5 us
    dot_general x16, matrix products, add_block(): lax.dot_general(weighted, low_hot, (((0,), (0,)), ((), ())), precision=la...  44.7 us
    all_to_all x1, waiting for transfers between devices, local(): lax.all_to_all(values, ('lat', 'lon'), split_axis=1, concat_axis=1, tiled...  29.4 us
    all_to_all x1, starting transfers between devices, local(): lax.all_to_all(values, ('lat', 'lon'), split_axis=1, concat_axis=1, tiled...  13.4 us
    mul x16, other arithmetic, add_block(): jnp.transpose(value_block)[:, :, None] * high_hot[:, None, :]  6.53 us
    ppermute x1, waiting for transfers between devices, exchange(): from_east = lax.ppermute(block[:, :, :width], 'lon', westward)  4.6 us
    unnamed x19, local copies, waits for them, and re-layouts  4.49 us
    ppermute x1, starting transfers between devices, exchange(): from_west = lax.ppermute(block[:, :, columns - width:], 'lon', eastward)  4.36 us
  transfers between devices with their start and end apart: 6, of which 3 were waited for; matrix products, arithmetic and copies ran while one was open for 3% of the time, Pallas kernels for 0%

profile of v1, /device:TPU:1, one launch (start us, length us, event | category | flops | bytes accessed | tf_op | source)
XLA Modules:
  0.0 206.4 jit_solution(11718326986018521394)
XLA Ops:
  0.6 0.7 bitcast_dynamic-update-slice_fusion.4
  1.4 0.7 bitcast_dynamic-update-slice_fusion.3
  2.1 0.7 bitcast_dynamic-update-slice_fusion.2
  2.8 0.7 bitcast_dynamic-update-slice_fusion.1
  3.5 0.9 constant_dynamic-update-slice_fusion
  4.6 4.4 %collective-permute-start = (f32[12,32,8]{2,1,0:T(8,128)S(1)}, f32[12,32,8]{2,1,0:T(8,128)S(1)}, u32[]{:S(2)}, u32[]{:S(2)}) collective-permute-start(f32[12,32,8]{2,1,0:T(8,128)S(1)} %get-tuple-element.262), channel_id=1, source_target_pairs={{0,1},{1,2},{2,3},{3,4},{4,5},{5,6},{6,7},{7,8},{8,9},{9,10},{10,1... | collective-permute-start | bytes 36872 | tf_op jit(solution)/shard_map/ppermute | solution.py:31
  8.9 0.8 iota_compare_fusion.8
  9.7 1.8 collective-permute-done
  11.5 4.6 %collective-permute-done.1 = f32[12,32,8]{2,1,0:T(8,128)S(1)} collective-permute-done((f32[12,32,8]{2,1,0:T(8,128)S(1)}, f32[12,32,8]{2,1,0:T(8,128)S(1)}, u32[]{:S(2)}, u32[]{:S(2)}) %collective-permute-start.1) | collective-permute-done | bytes 12320 | tf_op jit(solution)/shard_map/ppermute | solution.py:32
  16.1 0.8 pad_maximum_fusion.6
  17.0 1.3 collective-permute-start.4
  18.2 1.3 collective-permute-start.3
  19.7 1.1 reshape_reshape_squeeze.6
  20.8 4.3 %collective-permute-start.2 = (f32[12,8,144]{2,1,0:T(8,128)}, f32[12,8,144]{2,1,0:T(8,128)S(1)}, u32[]{:S(2)}, u32[]{:S(2)}) collective-permute-start(f32[12,8,144]{2,1,0:T(8,128)} %get-tuple-element.260), channel_id=1, source_target_pairs={{0,16},{16,32},{32,48},{48,64},{64,80},{80,96},{96,112},{1,17},{17... | collective-permute-start | bytes 165896 | tf_op jit(solution)/shard_map/ppermute | solution.py:37
  25.2 1.6 reverse
  26.7 1.0 multiply_select_fusion
  31.5 0.6 copy-done.1
  32.2 62.9 %while.26 = (s32[]{:T(128)}, f32[16,8192,4]{1,2,0:T(4,128)S(1)}, s32[16,8192]{1,0:T(8,128)S(1)}, f32[128,128]{1,0:T(8,128)S(1)}, s32[]{:T(128)}) while((s32[]{:T(128)}, f32[16,8192,4]{1,2,0:T(4,128)S(1)}, s32[16,8192]{1,0:T(8,128)S(1)}, f32[128,128]{1,0:T(8,128)S(1)}, s32[]{:T(128)}) %tuple.113), condition=%wide.region_2.3_spmd.clone, body=%wide.region_0.2_spmd.clone.sunk | while | flops 1614405632 | bytes 2785357 | solution.py:82
  32.4 3.7 %multiply_reduce_fusion.2 = f32[8192,4]{0,1:T(4,128)S(1)} fusion(f32[8192,32]{0,1:T(8,128)S(1)} %fusion.126, f32[128,128]{1,0:T(8,128)S(1)} %get-tuple-element.399, s32[8192]{0:T(1024)S(1)} %get-tuple-element.379), kind=kOutput, calls=%fused_computation.5.clone.1 | convolution fusion | flops 1613725696 | bytes 1277952 | tf_op jit(solution)/shard_map/while/body/eval_jaxpr/dot_general | solution.py:76
  36.3 3.7 %multiply_reduce_fusion.2 = f32[8192,4]{0,1:T(4,128)S(1)} fusion(f32[8192,32]{0,1:T(8,128)S(1)} %fusion.126, f32[128,128]{1,0:T(8,128)S(1)} %get-tuple-element.399, s32[8192]{0:T(1024)S(1)} %get-tuple-element.379), kind=kOutput, calls=%fused_computation.5.clone.1 | convolution fusion | flops 1613725696 | bytes 1277952 | tf_op jit(solution)/shard_map/while/body/eval_jaxpr/dot_general | solution.py:76
  40.3 3.7 %multiply_reduce_fusion.2 = f32[8192,4]{0,1:T(4,128)S(1)} fusion(f32[8192,32]{0,1:T(8,128)S(1)} %fusion.126, f32[128,128]{1,0:T(8,128)S(1)} %get-tuple-element.399, s32[8192]{0:T(1024)S(1)} %get-tuple-element.379), kind=kOutput, calls=%fused_computation.5.clone.1 | convolution fusion | flops 1613725696 | bytes 1277952 | tf_op jit(solution)/shard_map/while/body/eval_jaxpr/dot_general | solution.py:76
  44.2 3.7 %multiply_reduce_fusion.2 = f32[8192,4]{0,1:T(4,128)S(1)} fusion(f32[8192,32]{0,1:T(8,128)S(1)} %fusion.126, f32[128,128]{1,0:T(8,128)S(1)} %get-tuple-element.399, s32[8192]{0:T(1024)S(1)} %get-tuple-element.379), kind=kOutput, calls=%fused_computation.5.clone.1 | convolution fusion | flops 1613725696 | bytes 1277952 | tf_op jit(solution)/shard_map/while/body/eval_jaxpr/dot_general | solution.py:76
  48.1 3.7 %multiply_reduce_fusion.2 = f32[8192,4]{0,1:T(4,128)S(1)} fusion(f32[8192,32]{0,1:T(8,128)S(1)} %fusion.126, f32[128,128]{1,0:T(8,128)S(1)} %get-tuple-element.399, s32[8192]{0:T(1024)S(1)} %get-tuple-element.379), kind=kOutput, calls=%fused_computation.5.clone.1 | convolution fusion | flops 1613725696 | bytes 1277952 | tf_op jit(solution)/shard_map/while/body/eval_jaxpr/dot_general | solution.py:76
  52.1 3.7 %multiply_reduce_fusion.2 = f32[8192,4]{0,1:T(4,128)S(1)} fusion(f32[8192,32]{0,1:T(8,128)S(1)} %fusion.126, f32[128,128]{1,0:T(8,128)S(1)} %get-tuple-element.399, s32[8192]{0:T(1024)S(1)} %get-tuple-element.379), kind=kOutput, calls=%fused_computation.5.clone.1 | convolution fusion | flops 1613725696 | bytes 1277952 | tf_op jit(solution)/shard_map/while/body/eval_jaxpr/dot_general | solution.py:76
  56.0 3.7 %multiply_reduce_fusion.2 = f32[8192,4]{0,1:T(4,128)S(1)} fusion(f32[8192,32]{0,1:T(8,128)S(1)} %fusion.126, f32[128,128]{1,0:T(8,128)S(1)} %get-tuple-element.399, s32[8192]{0:T(1024)S(1)} %get-tuple-element.379), kind=kOutput, calls=%fused_computation.5.clone.1 | convolution fusion | flops 1613725696 | bytes 1277952 | tf_op jit(solution)/shard_map/while/body/eval_jaxpr/dot_general | solution.py:76
  59.9 3.7 %multiply_reduce_fusion.2 = f32[8192,4]{0,1:T(4,128)S(1)} fusion(f32[8192,32]{0,1:T(8,128)S(1)} %fusion.126, f32[128,128]{1,0:T(8,128)S(1)} %get-tuple-element.399, s32[8192]{0:T(1024)S(1)} %get-tuple-element.379), kind=kOutput, calls=%fused_computation.5.clone.1 | convolution fusion | flops 1613725696 | bytes 1277952 | tf_op jit(solution)/shard_map/while/body/eval_jaxpr/dot_general | solution.py:76
  63.9 3.7 %multiply_reduce_fusion.2 = f32[8192,4]{0,1:T(4,128)S(1)} fusion(f32[8192,32]{0,1:T(8,128)S(1)} %fusion.126, f32[128,128]{1,0:T(8,128)S(1)} %get-tuple-element.399, s32[8192]{0:T(1024)S(1)} %get-tuple-element.379), kind=kOutput, calls=%fused_computation.5.clone.1 | convolution fusion | flops 1613725696 | bytes 1277952 | tf_op jit(solution)/shard_map/while/body/eval_jaxpr/dot_general | solution.py:76
  67.8 3.7 %multiply_reduce_fusion.2 = f32[8192,4]{0,1:T(4,128)S(1)} fusion(f32[8192,32]{0,1:T(8,128)S(1)} %fusion.126, f32[128,128]{1,0:T(8,128)S(1)} %get-tuple-element.399, s32[8192]{0:T(1024)S(1)} %get-tuple-element.379), kind=kOutput, calls=%fused_computation.5.clone.1 | convolution fusion | flops 1613725696 | bytes 1277952 | tf_op jit(solution)/shard_map/while/body/eval_jaxpr/dot_general | solution.py:76
  71.7 3.7 %multiply_reduce_fusion.2 = f32[8192,4]{0,1:T(4,128)S(1)} fusion(f32[8192,32]{0,1:T(8,128)S(1)} %fusion.126, f32[128,128]{1,0:T(8,128)S(1)} %get-tuple-element.399, s32[8192]{0:T(1024)S(1)} %get-tuple-element.379), kind=kOutput, calls=%fused_computation.5.clone.1 | convolution fusion | flops 1613725696 | bytes 1277952 | tf_op jit(solution)/shard_map/while/body/eval_jaxpr/dot_general | solution.py:76
  75.7 3.7 %multiply_reduce_fusion.2 = f32[8192,4]{0,1:T(4,128)S(1)} fusion(f32[8192,32]{0,1:T(8,128)S(1)} %fusion.126, f32[128,128]{1,0:T(8,128)S(1)} %get-tuple-element.399, s32[8192]{0:T(1024)S(1)} %get-tuple-element.379), kind=kOutput, calls=%fused_computation.5.clone.1 | convolution fusion | flops 1613725696 | bytes 1277952 | tf_op jit(solution)/shard_map/while/body/eval_jaxpr/dot_general | solution.py:76
  79.6 3.7 %multiply_reduce_fusion.2 = f32[8192,4]{0,1:T(4,128)S(1)} fusion(f32[8192,32]{0,1:T(8,128)S(1)} %fusion.126, f32[128,128]{1,0:T(8,128)S(1)} %get-tuple-element.399, s32[8192]{0:T(1024)S(1)} %get-tuple-element.379), kind=kOutput, calls=%fused_computation.5.clone.1 | convolution fusion | flops 1613725696 | bytes 1277952 | tf_op jit(solution)/shard_map/while/body/eval_jaxpr/dot_general | solution.py:76
  83.5 3.7 %multiply_reduce_fusion.2 = f32[8192,4]{0,1:T(4,128)S(1)} fusion(f32[8192,32]{0,1:T(8,128)S(1)} %fusion.126, f32[128,128]{1,0:T(8,128)S(1)} %get-tuple-element.399, s32[8192]{0:T(1024)S(1)} %get-tuple-element.379), kind=kOutput, calls=%fused_computation.5.clone.1 | convolution fusion | flops 1613725696 | bytes 1277952 | tf_op jit(solution)/shard_map/while/body/eval_jaxpr/dot_general | solution.py:76
  87.5 3.7 %multiply_reduce_fusion.2 = f32[8192,4]{0,1:T(4,128)S(1)} fusion(f32[8192,32]{0,1:T(8,128)S(1)} %fusion.126, f32[128,128]{1,0:T(8,128)S(1)} %get-tuple-element.399, s32[8192]{0:T(1024)S(1)} %get-tuple-element.379), kind=kOutput, calls=%fused_computation.5.clone.1 | convolution fusion | flops 1613725696 | bytes 1277952 | tf_op jit(solution)/shard_map/while/body/eval_jaxpr/dot_general | solution.py:76
  91.4 3.7 %multiply_reduce_fusion.2 = f32[8192,4]{0,1:T(4,128)S(1)} fusion(f32[8192,32]{0,1:T(8,128)S(1)} %fusion.126, f32[128,128]{1,0:T(8,128)S(1)} %get-tuple-element.399, s32[8192]{0:T(1024)S(1)} %get-tuple-element.379), kind=kOutput, calls=%fused_computation.5.clone.1 | convolution fusion | flops 1613725696 | bytes 1277952 | tf_op jit(solution)/shard_map/while/body/eval_jaxpr/dot_general | solution.py:76
  95.2 2.4 %fusion.19 = f32[4,128,1024]{2,1,0:T(8,128)S(1)} fusion(f32[1,4,128,1024]{3,1,2,0:T(4,128)S(1)} %bitcast.100, f32[128,1024]{1,0:T(8,128)} %bitcast.101, pred[128,1024]{1,0:T(8,128)(4,1)S(1)} %iota_compare_fusion.8), kind=kLoop, calls=%fused_computation.39 | loop fusion | flops 1048576 | bytes 4849664 | tf_op jit(solution)/shard_map/jit(_where)/select_n | solution.py:195
  97.6 2.7 %copy.25 = f32[4,128,1024]{2,0,1:T(4,128)} copy(f32[4,128,1024]{2,1,0:T(8,128)S(1)} %fusion.19) | data formatting | bytes 4194304 | tf_op jit(solution)/shard_map/jit(_where)/select_n | solution.py:195
  100.3 13.4 %all-to-all-start = ((f32[4,128,1024]{2,0,1:T(4,128)}), f32[4,128,1024]{2,0,1:T(4,128)S(1)}, u32[]{:S(2)}, u32[]{:S(2)}) async-start(f32[4,128,1024]{2,0,1:T(4,128)} %copy.25), calls=%async_computation | async-start | bytes 4194304 | tf_op jit(solution)/shard_map/all_to_all | solution.py:197
  113.8 0.7 slice.437
  114.5 29.4 %all-to-all-done = f32[4,128,1024]{2,0,1:T(4,128)S(1)} async-done(((f32[4,128,1024]{2,0,1:T(4,128)}), f32[4,128,1024]{2,0,1:T(4,128)S(1)}, u32[]{:S(2)}, u32[]{:S(2)}) %all-to-all-start) | async-done | bytes 2097184 | tf_op jit(solution)/shard_map/all_to_all | solution.py:197
  143.9 2.6 %copy.26 = f32[4,128,1024]{2,1,0:T(8,128)} copy(f32[4,128,1024]{2,0,1:T(4,128)S(1)} %all-to-all-done) | data formatting | bytes 4194304 | tf_op jit(solution)/shard_map/all_to_all | solution.py:197
  146.4 1.7 reshape_reshape.3
  148.2 57.6 %while.27 = (s32[]{:T(128)}, f32[128,128]{1,0:T(8,128)S(1)}, f32[16,4,8192]{2,0,1:T(8,128)S(1)}, s32[16,8192]{1,0:T(8,128)S(1)}, s32[]{:T(128)}, /*index=5*/s32[]{:T(128)}) while((s32[]{:T(128)}, f32[128,128]{1,0:T(8,128)S(1)}, f32[16,4,8192]{2,0,1:T(8,128)S(1)}, s32[16,8192]{1,0:T(8,128)S(1)}, s32[]{:T(128)}, ...), condition=%wide.region_4.5_spmd.clone, body=%wide.region_3.4_spmd.clone.sunk | while | flops 1613422592 | bytes 11501663 | solution.py:113
  149.0 2.8 %fusion.129 = f32[128,128]{1,0:T(8,128)S(1)} fusion(f32[8192,128]{0,1:T(8,128)S(1)} %bitcast.95, s32[8192]{0:T(1024)S(1)} %get-tuple-element.385, f32[128,128]{1,0:T(8,128)S(1)} %get-tuple-element.408, pred[]{:T(512)S(6)} %compare.31), kind=kOutput, calls=%fused_computation.24.clone.1 | convolution fusion | flops 1611694080 | bytes 4358145 | tf_op jit(solution)/shard_map/while/body/eval_jaxpr/dot_general | solution.py:103
  152.2 0.4 broadcast_multiply_fusion.2
  152.6 2.8 %fusion.129 = f32[128,128]{1,0:T(8,128)S(1)} fusion(f32[8192,128]{0,1:T(8,128)S(1)} %bitcast.95, s32[8192]{0:T(1024)S(1)} %get-tuple-element.385, f32[128,128]{1,0:T(8,128)S(1)} %get-tuple-element.408, pred[]{:T(512)S(6)} %compare.31), kind=kOutput, calls=%fused_computation.24.clone.1 | convolution fusion | flops 1611694080 | bytes 4358145 | tf_op jit(solution)/shard_map/while/body/eval_jaxpr/dot_general | solution.py:103
  155.8 0.4 broadcast_multiply_fusion.2
  156.2 2.8 %fusion.129 = f32[128,128]{1,0:T(8,128)S(1)} fusion(f32[8192,128]{0,1:T(8,128)S(1)} %bitcast.95, s32[8192]{0:T(1024)S(1)} %get-tuple-element.385, f32[128,128]{1,0:T(8,128)S(1)} %get-tuple-element.408, pred[]{:T(512)S(6)} %compare.31), kind=kOutput, calls=%fused_computation.24.clone.1 | convolution fusion | flops 1611694080 | bytes 4358145 | tf_op jit(solution)/shard_map/while/body/eval_jaxpr/dot_general | solution.py:103
  159.4 0.4 broadcast_multiply_fusion.2
  159.8 2.8 %fusion.129 = f32[128,128]{1,0:T(8,128)S(1)} fusion(f32[8192,128]{0,1:T(8,128)S(1)} %bitcast.95, s32[8192]{0:T(1024)S(1)} %get-tuple-element.385, f32[128,128]{1,0:T(8,128)S(1)} %get-tuple-element.408, pred[]{:T(512)S(6)} %compare.31), kind=kOutput, calls=%fused_computation.24.clone.1 | convolution fusion | flops 1611694080 | bytes 4358145 | tf_op jit(solution)/shard_map/while/body/eval_jaxpr/dot_general | solution.py:103
  163.0 0.4 broadcast_multiply_fusion.2
  163.4 2.8 %fusion.129 = f32[128,128]{1,0:T(8,128)S(1)} fusion(f32[8192,128]{0,1:T(8,128)S(1)} %bitcast.95, s32[8192]{0:T(1024)S(1)} %get-tuple-element.385, f32[128,128]{1,0:T(8,128)S(1)} %get-tuple-element.408, pred[]{:T(512)S(6)} %compare.31), kind=kOutput, calls=%fused_computation.24.clone.1 | convolution fusion | flops 1611694080 | bytes 4358145 | tf_op jit(solution)/shard_map/while/body/eval_jaxpr/dot_general | solution.py:103
  166.6 0.4 broadcast_multiply_fusion.2
  167.0 2.8 %fusion.129 = f32[128,128]{1,0:T(8,128)S(1)} fusion(f32[8192,128]{0,1:T(8,128)S(1)} %bitcast.95, s32[8192]{0:T(1024)S(1)} %get-tuple-element.385, f32[128,128]{1,0:T(8,128)S(1)} %get-tuple-element.408, pred[]{:T(512)S(6)} %compare.31), kind=kOutput, calls=%fused_computation.24.clone.1 | convolution fusion | flops 1611694080 | bytes 4358145 | tf_op jit(solution)/shard_map/while/body/eval_jaxpr/dot_general | solution.py:103
  170.6 2.8 %fusion.129 = f32[128,128]{1,0:T(8,128)S(1)} fusion(f32[8192,128]{0,1:T(8,128)S(1)} %bitcast.95, s32[8192]{0:T(1024)S(1)} %get-tuple-element.385, f32[128,128]{1,0:T(8,128)S(1)} %get-tuple-element.408, pred[]{:T(512)S(6)} %compare.31), kind=kOutput, calls=%fused_computation.24.clone.1 | convolution fusion | flops 1611694080 | bytes 4358145 | tf_op jit(solution)/shard_map/while/body/eval_jaxpr/dot_general | solution.py:103
  174.2 2.8 %fusion.129 = f32[128,128]{1,0:T(8,128)S(1)} fusion(f32[8192,128]{0,1:T(8,128)S(1)} %bitcast.95, s32[8192]{0:T(1024)S(1)} %get-tuple-element.385, f32[128,128]{1,0:T(8,128)S(1)} %get-tuple-element.408, pred[]{:T(512)S(6)} %compare.31), kind=kOutput, calls=%fused_computation.24.clone.1 | convolution fusion | flops 1611694080 | bytes 4358145 | tf_op jit(solution)/shard_map/while/body/eval_jaxpr/dot_general | solution.py:103
  177.8 2.8 %fusion.129 = f32[128,128]{1,0:T(8,128)S(1)} fusion(f32[8192,128]{0,1:T(8,128)S(1)} %bitcast.95, s32[8192]{0:T(1024)S(1)} %get-tuple-element.385, f32[128,128]{1,0:T(8,128)S(1)} %get-tuple-element.408, pred[]{:T(512)S(6)} %compare.31), kind=kOutput, calls=%fused_computation.24.clone.1 | convolution fusion | flops 1611694080 | bytes 4358145 | tf_op jit(solution)/shard_map/while/body/eval_jaxpr/dot_general | solution.py:103
  181.4 2.8 %fusion.129 = f32[128,128]{1,0:T(8,128)S(1)} fusion(f32[8192,128]{0,1:T(8,128)S(1)} %bitcast.95, s32[8192]{0:T(1024)S(1)} %get-tuple-element.385, f32[128,128]{1,0:T(8,128)S(1)} %get-tuple-element.408, pred[]{:T(512)S(6)} %compare.31), kind=kOutput, calls=%fused_computation.24.clone.1 | convolution fusion | flops 1611694080 | bytes 4358145 | tf_op jit(solution)/shard_map/while/body/eval_jaxpr/dot_general | solution.py:103
  185.0 2.8 %fusion.129 = f32[128,128]{1,0:T(8,128)S(1)} fusion(f32[8192,128]{0,1:T(8,128)S(1)} %bitcast.95, s32[8192]{0:T(1024)S(1)} %get-tuple-element.385, f32[128,128]{1,0:T(8,128)S(1)} %get-tuple-element.408, pred[]{:T(512)S(6)} %compare.31), kind=kOutput, calls=%fused_computation.24.clone.1 | convolution fusion | flops 1611694080 | bytes 4358145 | tf_op jit(solution)/shard_map/while/body/eval_jaxpr/dot_general | solution.py:103
  188.6 2.8 %fusion.129 = f32[128,128]{1,0:T(8,128)S(1)} fusion(f32[8192,128]{0,1:T(8,128)S(1)} %bitcast.95, s32[8192]{0:T(1024)S(1)} %get-tuple-element.385, f32[128,128]{1,0:T(8,128)S(1)} %get-tuple-element.408, pred[]{:T(512)S(6)} %compare.31), kind=kOutput, calls=%fused_computation.24.clone.1 | convolution fusion | flops 1611694080 | bytes 4358145 | tf_op jit(solution)/shard_map/while/body/eval_jaxpr/dot_general | solution.py:103
  192.2 2.8 %fusion.129 = f32[128,128]{1,0:T(8,128)S(1)} fusion(f32[8192,128]{0,1:T(8,128)S(1)} %bitcast.95, s32[8192]{0:T(1024)S(1)} %get-tuple-element.385, f32[128,128]{1,0:T(8,128)S(1)} %get-tuple-element.408, pred[]{:T(512)S(6)} %compare.31), kind=kOutput, calls=%fused_computation.24.clone.1 | convolution fusion | flops 1611694080 | bytes 4358145 | tf_op jit(solution)/shard_map/while/body/eval_jaxpr/dot_general | solution.py:103
  195.8 2.8 %fusion.129 = f32[128,128]{1,0:T(8,128)S(1)} fusion(f32[8192,128]{0,1:T(8,128)S(1)} %bitcast.95, s32[8192]{0:T(1024)S(1)} %get-tuple-element.385, f32[128,128]{1,0:T(8,128)S(1)} %get-tuple-element.408, pred[]{:T(512)S(6)} %compare.31), kind=kOutput, calls=%fused_computation.24.clone.1 | convolution fusion | flops 1611694080 | bytes 4358145 | tf_op jit(solution)/shard_map/while/body/eval_jaxpr/dot_general | solution.py:103
  199.4 2.8 %fusion.129 = f32[128,128]{1,0:T(8,128)S(1)} fusion(f32[8192,128]{0,1:T(8,128)S(1)} %bitcast.95, s32[8192]{0:T(1024)S(1)} %get-tuple-element.385, f32[128,128]{1,0:T(8,128)S(1)} %get-tuple-element.408, pred[]{:T(512)S(6)} %compare.31), kind=kOutput, calls=%fused_computation.24.clone.1 | convolution fusion | flops 1611694080 | bytes 4358145 | tf_op jit(solution)/shard_map/while/body/eval_jaxpr/dot_general | solution.py:103
  203.0 2.8 %fusion.129 = f32[128,128]{1,0:T(8,128)S(1)} fusion(f32[8192,128]{0,1:T(8,128)S(1)} %bitcast.95, s32[8192]{0:T(1024)S(1)} %get-tuple-element.385, f32[128,128]{1,0:T(8,128)S(1)} %get-tuple-element.408, pred[]{:T(512)S(6)} %compare.31), kind=kOutput, calls=%fused_computation.24.clone.1 | convolution fusion | flops 1611694080 | bytes 4358145 | tf_op jit(solution)/shard_map/while/body/eval_jaxpr/dot_general | solution.py:103
  205.8 0.7 reshape.327
  (233 shorter events, 16.0 us)
Async XLA Ops:
  0.6 26.1 %copy-start.6 = (f32[12]{0:T(128)S(1)}, f32[12]{0:T(128)}, u32[]{:S(2)}) copy-start(f32[12]{0:T(128)} %constant.170.clone) | copy-start | bytes 148
  4.6 7.0 %collective-permute-start = (f32[12,32,8]{2,1,0:T(8,128)S(1)}, f32[12,32,8]{2,1,0:T(8,128)S(1)}, u32[]{:S(2)}, u32[]{:S(2)}) collective-permute-start(f32[12,32,8]{2,1,0:T(8,128)S(1)} %get-tuple-element.262), channel_id=1, source_target_pairs={{0,1},{1,2},{2,3},{3,4},{4,5},{5,6},{6,7},{7,8},{8,9},{9,10},{10,1... | collective-permute-start | bytes 36872 | tf_op jit(solution)/shard_map/ppermute | solution.py:31
  8.9 7.2 %collective-permute-start.1 = (f32[12,32,8]{2,1,0:T(8,128)S(1)}, f32[12,32,8]{2,1,0:T(8,128)S(1)}, u32[]{:S(2)}, u32[]{:S(2)}) collective-permute-start(f32[12,32,8]{2,1,0:T(8,128)S(1)} %get-tuple-element.263), channel_id=1, source_target_pairs={{1,0},{2,1},{3,2},{4,3},{5,4},{6,5},{7,6},{8,7},{9,8},{10,9},{11,1... | collective-permute-start | bytes 36872 | tf_op jit(solution)/shard_map/ppermute | solution.py:32
  17.0 9.8 %collective-permute-start.4 = (f32[12,8,144]{2,1,0:T(8,128)}, f32[12,8,144]{2,1,0:T(8,128)}, u32[]{:S(2)}, u32[]{:S(2)}) collective-permute-start(f32[12,8,144]{2,1,0:T(8,128)} %get-tuple-element.261), channel_id=1, source_target_pairs={{16,0},{32,16},{48,32},{64,48},{80,64},{96,80},{112,96},{17,1},{33... | collective-permute-start | bytes 165896 | tf_op jit(solution)/shard_map/ppermute | solution.py:38
  18.2 6.9 %collective-permute-start.3 = (f32[12,8,144]{2,1,0:T(8,128)}, f32[12,8,144]{2,1,0:T(8,128)}, u32[]{:S(2)}, u32[]{:S(2)}) collective-permute-start(f32[12,8,144]{2,1,0:T(8,128)} %get-tuple-element.260), channel_id=1, source_target_pairs={{112,127},{113,126},{114,125},{115,124},{116,123},{117,122},{118,1... | collective-permute-start | bytes 165896 | tf_op jit(solution)/shard_map/ppermute | solution.py:41
  20.8 7.0 %collective-permute-start.2 = (f32[12,8,144]{2,1,0:T(8,128)}, f32[12,8,144]{2,1,0:T(8,128)S(1)}, u32[]{:S(2)}, u32[]{:S(2)}) collective-permute-start(f32[12,8,144]{2,1,0:T(8,128)} %get-tuple-element.260), channel_id=1, source_target_pairs={{0,16},{16,32},{32,48},{48,64},{64,80},{80,96},{96,112},{1,17},{17... | collective-permute-start | bytes 165896 | tf_op jit(solution)/shard_map/ppermute | solution.py:37
  29.9 1.2 copy-start.2
  29.9 1.2 copy-start.3
  30.8 1.5 copy-start.4
  30.8 1.4 copy-start.5
  31.4 0.7 copy-start.1
  100.3 13.4 %copy-start = (s32[1,128,1024]{2,1,0:T(8,128)S(1)}, s32[1,128,1024]{2,1,0:T(8,128)}, u32[]{:S(2)}) copy-start(s32[1,128,1024]{2,1,0:T(8,128)} %param.26) | copy-start | bytes 1572868
  100.3 43.6 %all-to-all-start = ((f32[4,128,1024]{2,0,1:T(4,128)}), f32[4,128,1024]{2,0,1:T(4,128)S(1)}, u32[]{:S(2)}, u32[]{:S(2)}) async-start(f32[4,128,1024]{2,0,1:T(4,128)} %copy.25), calls=%async_computation | async-start | bytes 4194304 | tf_op jit(solution)/shard_map/all_to_all | solution.py:197

commit v2 on v1

--- a/solution.py
+++ b/solution.py
@@ -3,6 +3,7 @@
 import jax
 import jax.numpy as jnp
 from jax import lax
+from jax.experimental import pallas as pl
 from jax.sharding import PartitionSpec as P
 
 VERTICAL_STRATA = 8
@@ -16,7 +17,6 @@
 spin_coef = 0.3
 mix_coef = 0.1
 carry_coef = 0.1
-block_limit = 8192
 
 
 HALO = 2 * STEPS
@@ -61,56 +61,104 @@
     return jnp.concatenate([x[..., :1, :], x[..., :-1, :]], axis=-2)
 
 
-def pick_cells(surface_grid, indices):
+GROUP = 8
+
+
+def split_pieces(x):
+    high = x.astype(jnp.bfloat16)
+    low = (x - high.astype(jnp.float32)).astype(jnp.bfloat16)
+    return high, low
+
+
+def pick_kernel(table_ref, index_ref, extent_ref, tally_ref, out_ref):
+    fields_count = out_ref.shape[0]
+    slots = index_ref.shape[1]
+    table_rows = table_ref.shape[0]
+    columns = table_ref.shape[1]
+    rows = table_rows // fields_count
+    table = jnp.concatenate(split_pieces(table_ref[...]), axis=1)
+    column_ids = lax.broadcasted_iota(jnp.int32, (columns, slots), 0)
+    row_ids = lax.broadcasted_iota(jnp.int32, (rows, slots), 0)
+    slot_ids = lax.broadcasted_iota(jnp.int32, (1, slots), 1)
+    for owner in range(index_ref.shape[0]):
+        index = index_ref[pl.ds(owner, 1), :]
+        hot = (column_ids == index % columns).astype(jnp.bfloat16)
+        by_column = jnp.dot(
+            table, jnp.concatenate([hot, hot], axis=0), preferred_element_type=jnp.float32
+        )
+        row_hot = row_ids == index // columns
+        weight = jnp.where(
+            slot_ids < tally_ref[pl.ds(owner, 1), :], extent_ref[pl.ds(owner, 1), :], 0.0
+        )
+        for field in range(fields_count):
+            part = by_column[field * rows : (field + 1) * rows]
+            picked = jnp.sum(jnp.where(row_hot, part, 0.0), axis=0, keepdims=True)
+            out_ref[field, pl.ds(owner, 1), :] = picked * weight
+
+
+def pick_cells(surface_grid, indices, extent, tally):
     fields_count, rows, columns = surface_grid.shape
-    table = jnp.transpose(surface_grid, (2, 0, 1)).reshape(columns, fields_count * rows)
-    total = indices.shape[0]
-    size = math.gcd(total, block_limit)
-    blocks = indices.reshape(total // size, size)
-    column_ids = jnp.arange(columns)
-    row_ids = jnp.arange(rows)
-
-    def one_block(block):
-        column_hot = (block[:, None] % columns == column_ids[None, :]).astype(jnp.float32)
-        row_hot = (block[:, None] // columns == row_ids[None, :]).astype(jnp.float32)
-        by_column = jnp.dot(
-            column_hot, table, precision=lax.Precision.HIGHEST, preferred_element_type=jnp.float32
+    owners, slots = indices.shape
+    table = surface_grid.reshape(fields_count * rows, columns)
+    return pl.pallas_call(
+        pick_kernel,
+        out_shape=jax.ShapeDtypeStruct((fields_count, owners, slots), jnp.float32),
+        grid=(owners // GROUP,),
+        in_specs=[
+            pl.BlockSpec((fields_count * rows, columns), lambda i: (0, 0)),
+            pl.BlockSpec((GROUP, slots), lambda i: (i, 0)),
+            pl.BlockSpec((GROUP, slots), lambda i: (i, 0)),
+            pl.BlockSpec((GROUP, 1), lambda i: (i, 0)),
+        ],
+        out_specs=pl.BlockSpec((fields_count, GROUP, slots), lambda i: (0, i, 0)),
+    )(table, indices, extent, tally[:, None])
+
+
+def spread_kernel(value_ref, target_ref, out_ref):
+    fields_count = value_ref.shape[0]
+    slots = value_ref.shape[2]
+    lows = out_ref.shape[1]
+    highs = out_ref.shape[0] // fields_count
+
+    @pl.when(pl.program_id(0) == 0)
+    def _():
+        out_ref[...] = jnp.zeros_like(out_ref)
+
+    high_ids = lax.broadcasted_iota(jnp.int32, (highs, slots), 0)
+    low_ids = lax.broadcasted_iota(jnp.int32, (lows, slots), 0)
+    total = jnp.zeros(out_ref.shape, jnp.float32)
+    for sender in range(target_ref.shape[0]):
+        target = target_ref[pl.ds(sender, 1), :]
+        high_hot = high_ids == target // lows
+        low_hot = (low_ids == target % lows).astype(jnp.bfloat16)
+        weighted = jnp.concatenate(
+            [
+                jnp.where(high_hot, value_ref[field, pl.ds(sender, 1), :], 0.0)
+                for field in range(fields_count)
+            ],
+            axis=0,
         )
-        by_column = by_column.reshape(size, fields_count, rows)
-        return jnp.sum(by_column * row_hot[:, None, :], axis=2)
-
-    picked = lax.map(one_block, blocks).reshape(total, fields_count)
-    return jnp.transpose(picked)
+        for piece in split_pieces(weighted):
+            total = total + lax.dot_general(
+                piece, low_hot, (((1,), (1,)), ((), ())), preferred_element_type=jnp.float32
+            )
+    out_ref[...] += total
 
 
 def spread_cells(values, targets, cells):
-    fields_count = values.shape[0]
-    total = targets.shape[0]
-    size = math.gcd(total, block_limit)
-    high_count = cells // 128
-    value_blocks = jnp.transpose(values.reshape(fields_count, total // size, size), (1, 0, 2))
-    target_blocks = targets.reshape(total // size, size)
-    low_ids = jnp.arange(128)
-    high_ids = jnp.arange(high_count)
-
-    def add_block(carry, pieces):
-        value_block, target_block = pieces
-        low_hot = (target_block[:, None] % 128 == low_ids[None, :]).astype(jnp.float32)
-        high_hot = (target_block[:, None] // 128 == high_ids[None, :]).astype(jnp.float32)
-        weighted = (jnp.transpose(value_block)[:, :, None] * high_hot[:, None, :]).reshape(
-            size, fields_count * high_count
-        )
-        term = lax.dot_general(
-            weighted,
-            low_hot,
-            (((0,), (0,)), ((), ())),
-            precision=lax.Precision.HIGHEST,
-            preferred_element_type=jnp.float32,
-        )
-        return (carry + term, None)
-
-    start = jnp.zeros((fields_count * high_count, 128), jnp.float32)
-    summed, _ = lax.scan(add_block, start, (value_blocks, target_blocks))
+    fields_count, senders, slots = values.shape
+    lows = 256
+    highs = cells // lows
+    summed = pl.pallas_call(
+        spread_kernel,
+        out_shape=jax.ShapeDtypeStruct((fields_count * highs, lows), jnp.float32),
+        grid=(senders // GROUP,),
+        in_specs=[
+            pl.BlockSpec((fields_count, GROUP, slots), lambda i: (0, i, 0)),
+            pl.BlockSpec((GROUP, slots), lambda i: (i, 0)),
+        ],
+        out_specs=pl.BlockSpec((fields_count * highs, lows), lambda i: (0, 0)),
+    )(values, targets)
     return summed.reshape(fields_count, cells)
 
 
@@ -186,17 +234,11 @@
         passive_scalar_values + mix_coef * mixing - carry_coef * carried
     )
     surface_grid = jnp.stack([height, speed_east[0], speed_north[0], tracer_new[0]])
-    owners = sent_sender_mesh_index.shape[1]
-    slots = sent_sender_mesh_index.shape[2]
-    picked = pick_cells(surface_grid, sent_sender_mesh_index[0].reshape(-1)).reshape(
-        NF, owners, slots
-    )
-    live = jnp.arange(slots)[None, :] < sent_entry_tally[0][:, None]
-    values = jnp.where(live[None], sent_intersection_extent[0][None] * picked, 0.0)
-    targets = received_atmosphere_mesh_index[0].reshape(-1)
+    values = pick_cells(
+        surface_grid, sent_sender_mesh_index[0], sent_intersection_extent[0], sent_entry_tally[0]
+    )
     block = lax.all_to_all(values, ("lat", "lon"), split_axis=1, concat_axis=1, tiled=True)
-    fields_count = block.shape[0]
-    atmosphere = spread_cells(block.reshape(fields_count, -1), targets, ACELL)
+    atmosphere = spread_cells(block, received_atmosphere_mesh_index[0], ACELL)
     return (height, east, north, tracer_new, atmosphere)
 
 

time: 207 us -> 158 us (0.76)
  matrix products: 104 us -> 0 us
  Pallas kernels: 0 us -> 74.9 us
  other arithmetic: 17.7 us -> 3.64 us
  local copies, waits for them, and re-layouts: 20.9 us -> 15.3 us
  waiting for transfers between devices: 35.8 us -> 38.1 us
    dot_general x32 -> x0, matrix products: 104 us -> none  [the longest x16 59.5 us: one_block(): jnp.dot(column_hot, table, precision=lax.Precision.HIGHEST, preferred_ele...]
    pallas_call x0 -> x2, Pallas kernels: none -> 74.9 us  [the longest x1 46.4 us: spread_cells(): pl.pallas_call(spread_kernel, out_shape=jax.ShapeDtypeStruct((fields_coun...]
    mul x16 -> x0, other arithmetic: 6.53 us -> none  [add_block(): jnp.transpose(value_block)[:, :, None] * high_hot[:, None, :]]
    pallas_call x0 -> x1, local copies, waits for them, and re-layouts: none -> 4.29 us  [pick_cells(): pl.pallas_call(pick_kernel, out_shape=jax.ShapeDtypeStruct((fields_count,...]
    dynamic_slice x64 -> x0, local copies, waits for them, and re-layouts: 3.99 us -> none  [the longest x32 3.01 us: spread_cells(): summed, _ = lax.scan(add_block, start, (value_blocks, target_blocks))]
    select_n x33 -> x0, other arithmetic: 3.45 us -> none  [the longest x1 2.42 us: local(): jnp.where(live[None], sent_intersection_extent[0][None] * picked, 0.0)]
    select_n x1 -> x0, local copies, waits for them, and re-layouts: 2.7 us -> none  [local(): jnp.where(live[None], sent_intersection_extent[0][None] * picked, 0.0)]
    convert_element_type x32 -> x0, other arithmetic: 2.31 us -> none  [the longest x16 1.15 us: one_block(): (block[:, None] // columns == row_ids[None, :]).astype(jnp.float32)]
  transfers between devices with their start and end apart: 6 -> 6, of which waited for: 3 -> 4; matrix products, arithmetic and copies ran while one was open for 3% -> 2% of each run, Pallas kernels for 0% -> 0%
where the time goes in v2:
time: 158 us; the launch traced here: 157 us
  Pallas kernels  74.9 us (47%)
  waiting for transfers between devices  38.1 us (24%)
  starting transfers between devices  24 us (15%)
  local copies, waits for them, and re-layouts  15.3 us (10%)
  other arithmetic  3.64 us (2%)
    pallas_call x1, Pallas kernels, spread_cells(): pl.pallas_call(spread_kernel, out_shape=jax.ShapeDtypeStruct((fields_coun...  46.4 us
    all_to_all x1, waiting for transfers between devices, local(): lax.all_to_all(values, ('lat', 'lon'), split_axis=1, concat_axis=1, tiled...  29.5 us
    pallas_call x1, Pallas kernels, pick_cells(): pl.pallas_call(pick_kernel, out_shape=jax.ShapeDtypeStruct((fields_count,...  28.5 us
    all_to_all x1, starting transfers between devices, local(): lax.all_to_all(values, ('lat', 'lon'), split_axis=1, concat_axis=1, tiled...  13.4 us
    ppermute x1, waiting for transfers between devices, exchange(): from_east = lax.ppermute(block[:, :, :width], 'lon', westward)  4.6 us
    ppermute x1, starting transfers between devices, exchange(): from_west = lax.ppermute(block[:, :, columns - width:], 'lon', eastward)  4.36 us
    pallas_call x1, local copies, waits for them, and re-layouts, pick_cells(): pl.pallas_call(pick_kernel, out_shape=jax.ShapeDtypeStruct((fields_count,...  4.29 us
    ppermute x1, starting transfers between devices, exchange(): from_south = lax.ppermute(top, 'lat', upward)  4.27 us
  transfers between devices with their start and end apart: 6, of which 4 were waited for; matrix products, arithmetic and copies ran while one was open for 2% of the time, Pallas kernels for 0%

profile of v2, /device:TPU:1, one launch (start us, length us, event | category | flops | bytes accessed | tf_op | source)
XLA Modules:
  0.0 156.9 jit_solution(12202235069040030491)
XLA Ops:
  0.6 0.7 bitcast_dynamic-update-slice_fusion.3
  1.4 0.7 bitcast_dynamic-update-slice_fusion.2
  2.1 0.7 bitcast_dynamic-update-slice_fusion.1
  2.8 0.7 bitcast_dynamic-update-slice_fusion
  3.5 0.9 constant_dynamic-update-slice_fusion
  4.4 0.1 fusion.65
  4.6 4.4 %collective-permute-start = (f32[12,32,8]{2,1,0:T(8,128)S(1)}, f32[12,32,8]{2,1,0:T(8,128)S(1)}, u32[]{:S(2)}, u32[]{:S(2)}) collective-permute-start(f32[12,32,8]{2,1,0:T(8,128)S(1)} %get-tuple-element.22), channel_id=1, source_target_pairs={{0,1},{1,2},{2,3},{3,4},{4,5},{5,6},{6,7},{7,8},{8,9},{9,10},{10,1... | collective-permute-start | bytes 36872 | tf_op jit(solution)/shard_map/ppermute | solution.py:31
  8.9 2.6 %collective-permute-done = f32[12,32,8]{2,1,0:T(8,128)S(1)} collective-permute-done((f32[12,32,8]{2,1,0:T(8,128)S(1)}, f32[12,32,8]{2,1,0:T(8,128)S(1)}, u32[]{:S(2)}, u32[]{:S(2)}) %collective-permute-start) | collective-permute-done | bytes 12320 | tf_op jit(solution)/shard_map/ppermute | solution.py:31
  11.5 4.6 %collective-permute-done.1 = f32[12,32,8]{2,1,0:T(8,128)S(1)} collective-permute-done((f32[12,32,8]{2,1,0:T(8,128)S(1)}, f32[12,32,8]{2,1,0:T(8,128)S(1)}, u32[]{:S(2)}, u32[]{:S(2)}) %collective-permute-start.1) | collective-permute-done | bytes 12320 | tf_op jit(solution)/shard_map/ppermute | solution.py:32
  16.1 0.1 pad_maximum_fusion.6
  16.3 1.3 collective-permute-start.4
  17.6 0.7 collective-permute-start.3
  18.3 0.1 fusion.61
  18.3 0.1 slice.449
  18.4 1.4 copy.18.tally_ref
  19.8 4.3 %collective-permute-start.2 = (f32[12,8,144]{2,1,0:T(8,128)S(1)}, f32[12,8,144]{2,1,0:T(8,128)S(1)}, u32[]{:S(2)}, u32[]{:S(2)}) collective-permute-start(f32[12,8,144]{2,1,0:T(8,128)S(1)} %get-tuple-element.20), channel_id=1, source_target_pairs={{0,16},{16,32},{32,48},{48,64},{64,80},{80,96},{96,112},{1,17},{17... | collective-permute-start | bytes 165896 | tf_op jit(solution)/shard_map/ppermute | solution.py:37
  24.1 0.2 reverse
  24.3 0.1 multiply_select_fusion
  24.4 1.4 collective-permute-done.2
  25.8 0.1 multiply_bitcast_fusion
  25.9 0.1 fusion.7
  25.9 0.1 fusion.8
  26.0 0.1 fusion.96
  26.1 0.1 fusion.97
  26.2 0.1 fusion.11
  26.3 0.1 fusion.91
  26.4 0.1 fusion.90
  26.5 0.1 fusion.25
  26.6 0.1 fusion.88
  26.7 0.1 fusion.89
  26.8 0.1 fusion.21
  26.9 0.1 fusion.83
  27.0 0.1 fusion.82
  27.1 0.1 fusion.37
  27.2 0.1 fusion.80
  27.3 0.1 fusion.81
  27.4 0.1 fusion.33
  27.5 0.1 fusion.75
  27.6 0.1 fusion.74
  27.7 0.1 fusion.49
  27.8 0.1 fusion.72
  27.9 0.1 fusion.73
  28.0 0.1 fusion.45
  28.1 0.1 slice_bitcast_fusion
  28.1 0.1 fusion.66
  28.2 0.1 fusion.67
  28.3 0.1 maximum_bitcast_fusion.3
  28.4 0.1 compare_convert_fusion
  28.5 0.1 fusion.53
  28.6 0.1 fusion.55
  28.7 0.0 copy-start.3
  28.7 0.0 copy-start.4
  28.7 0.3 compare_select_fusion
  29.0 0.3 fusion.4
  29.4 0.0 copy-start
  29.4 0.6 pad_maximum_fusion.7
  30.1 28.5 %shard_map.155 = f32[4,128,1024]{2,1,0:T(8,128)} custom-call(f32[128,128]{1,0:T(8,128)} %bitcast.59, s32[128,1024]{1,0:T(8,128)} %bitcast.56, f32[128,1024]{1,0:T(8,128)} %bitcast.57, s32[128,1]{1,0:T(8,128)} %copy.18.tally_ref), custom_call_target="tpu_custom_call" | custom-call | tf_op jit(solution)/shard_map/pallas_call | solution.py:103
  58.6 4.3 %copy.19 = f32[4,128,1024]{2,0,1:T(4,128)} copy(f32[4,128,1024]{2,1,0:T(8,128)} %shard_map.155) | data formatting | bytes 4194304 | tf_op jit(solution)/shard_map/pallas_call | solution.py:103
  62.9 13.4 %all-to-all-start = ((f32[4,128,1024]{2,0,1:T(4,128)}), f32[4,128,1024]{2,0,1:T(4,128)S(1)}, u32[]{:S(2)}, u32[]{:S(2)}) async-start(f32[4,128,1024]{2,0,1:T(4,128)} %copy.19), calls=%async_computation | async-start | bytes 4194304 | tf_op jit(solution)/shard_map/all_to_all | solution.py:240
  76.3 0.7 slice.437
  77.0 29.5 %all-to-all-done = f32[4,128,1024]{2,0,1:T(4,128)S(1)} async-done(((f32[4,128,1024]{2,0,1:T(4,128)}), f32[4,128,1024]{2,0,1:T(4,128)S(1)}, u32[]{:S(2)}, u32[]{:S(2)}) %all-to-all-start) | async-done | bytes 2097184 | tf_op jit(solution)/shard_map/all_to_all | solution.py:240
  106.5 2.5 %copy.20.value_ref = f32[4,128,1024]{2,1,0:T(8,128)} copy(f32[4,128,1024]{2,0,1:T(4,128)S(1)} %all-to-all-done) | data formatting | bytes 4194304 | tf_op jit(solution)/shard_map/all_to_all | solution.py:240
  109.0 46.4 %shard_map.156 = f32[64,256]{1,0:T(8,128)} custom-call(f32[4,128,1024]{2,1,0:T(8,128)} %copy.20.value_ref, s32[128,1024]{1,0:T(8,128)} %bitcast.58), custom_call_target="tpu_custom_call" | custom-call | tf_op jit(solution)/shard_map/pallas_call | solution.py:152
  155.4 1.5 reshape.40
  (32 shorter events, 0.2 us)
Async XLA Ops:
  0.6 23.6 %copy-start.5 = (f32[12]{0:T(128)S(1)}, f32[12]{0:T(128)}, u32[]{:S(2)}) copy-start(f32[12]{0:T(128)} %constant.54.clone) | copy-start | bytes 148
  4.6 7.0 %collective-permute-start = (f32[12,32,8]{2,1,0:T(8,128)S(1)}, f32[12,32,8]{2,1,0:T(8,128)S(1)}, u32[]{:S(2)}, u32[]{:S(2)}) collective-permute-start(f32[12,32,8]{2,1,0:T(8,128)S(1)} %get-tuple-element.22), channel_id=1, source_target_pairs={{0,1},{1,2},{2,3},{3,4},{4,5},{5,6},{6,7},{7,8},{8,9},{9,10},{10,1... | collective-permute-start | bytes 36872 | tf_op jit(solution)/shard_map/ppermute | solution.py:31
  8.9 7.2 %collective-permute-start.1 = (f32[12,32,8]{2,1,0:T(8,128)S(1)}, f32[12,32,8]{2,1,0:T(8,128)S(1)}, u32[]{:S(2)}, u32[]{:S(2)}) collective-permute-start(f32[12,32,8]{2,1,0:T(8,128)S(1)} %get-tuple-element.23), channel_id=1, source_target_pairs={{1,0},{2,1},{3,2},{4,3},{5,4},{6,5},{7,6},{8,7},{9,8},{10,9},{11,1... | collective-permute-start | bytes 36872 | tf_op jit(solution)/shard_map/ppermute | solution.py:32
  16.3 8.0 %collective-permute-start.4 = (f32[12,8,144]{2,1,0:T(8,128)S(1)}, f32[12,8,144]{2,1,0:T(8,128)S(1)}, u32[]{:S(2)}, u32[]{:S(2)}) collective-permute-start(f32[12,8,144]{2,1,0:T(8,128)S(1)} %get-tuple-element.21), channel_id=1, source_target_pairs={{16,0},{32,16},{48,32},{64,48},{80,64},{96,80},{112,96},{17,1},{33... | collective-permute-start | bytes 165896 | tf_op jit(solution)/shard_map/ppermute | solution.py:38
  17.6 6.5 %collective-permute-start.3 = (f32[12,8,144]{2,1,0:T(8,128)S(1)}, f32[12,8,144]{2,1,0:T(8,128)S(1)}, u32[]{:S(2)}, u32[]{:S(2)}) collective-permute-start(f32[12,8,144]{2,1,0:T(8,128)S(1)} %get-tuple-element.20), channel_id=1, source_target_pairs={{112,127},{113,126},{114,125},{115,124},{116,123},{117,122},{118,1... | collective-permute-start | bytes 165896 | tf_op jit(solution)/shard_map/ppermute | solution.py:41
  19.8 6.0 %collective-permute-start.2 = (f32[12,8,144]{2,1,0:T(8,128)S(1)}, f32[12,8,144]{2,1,0:T(8,128)S(1)}, u32[]{:S(2)}, u32[]{:S(2)}) collective-permute-start(f32[12,8,144]{2,1,0:T(8,128)S(1)} %get-tuple-element.20), channel_id=1, source_target_pairs={{0,16},{16,32},{32,48},{48,64},{64,80},{80,96},{96,112},{1,17},{17... | collective-permute-start | bytes 165896 | tf_op jit(solution)/shard_map/ppermute | solution.py:37
  27.8 1.2 copy-start.1
  27.8 1.2 copy-start.2
  28.7 29.9 %copy-start.3 = (f32[32,128]{1,0:T(8,128)}, f32[32,128]{1,0:T(8,128)S(1)}, u32[]{:S(2)}) copy-start(f32[32,128]{1,0:T(8,128)S(1)} %get-tuple-element.8) | copy-start | bytes 49156
  28.7 29.9 %copy-start.4 = (f32[32,128]{1,0:T(8,128)}, f32[32,128]{1,0:T(8,128)S(1)}, u32[]{:S(2)}) copy-start(f32[32,128]{1,0:T(8,128)S(1)} %get-tuple-element.9) | copy-start | bytes 49156
  29.4 33.5 %copy-start = (f32[8,32,128]{2,1,0:T(8,128)}, f32[8,32,128]{2,1,0:T(8,128)S(1)}, u32[]{:S(2)}) copy-start(f32[8,32,128]{2,1,0:T(8,128)S(1)} %get-tuple-element.5) | copy-start | bytes 393220
  62.9 43.6 %all-to-all-start = ((f32[4,128,1024]{2,0,1:T(4,128)}), f32[4,128,1024]{2,0,1:T(4,128)S(1)}, u32[]{:S(2)}, u32[]{:S(2)}) async-start(f32[4,128,1024]{2,0,1:T(4,128)} %copy.19), calls=%async_computation | async-start | bytes 4194304 | tf_op jit(solution)/shard_map/all_to_all | solution.py:240

commit v3 on v2

--- a/solution.py
+++ b/solution.py
@@ -78,7 +78,7 @@
     rows = table_rows // fields_count
     table = jnp.concatenate(split_pieces(table_ref[...]), axis=1)
     column_ids = lax.broadcasted_iota(jnp.int32, (columns, slots), 0)
-    row_ids = lax.broadcasted_iota(jnp.int32, (rows, slots), 0)
+    row_ids = lax.broadcasted_iota(jnp.int32, (8, slots), 0)
     slot_ids = lax.broadcasted_iota(jnp.int32, (1, slots), 1)
     for owner in range(index_ref.shape[0]):
         index = index_ref[pl.ds(owner, 1), :]
@@ -86,13 +86,17 @@
         by_column = jnp.dot(
             table, jnp.concatenate([hot, hot], axis=0), preferred_element_type=jnp.float32
         )
-        row_hot = row_ids == index // columns
+        row = index // columns
+        masks = [row_ids + 8 * tile == row for tile in range(rows // 8)]
         weight = jnp.where(
             slot_ids < tally_ref[pl.ds(owner, 1), :], extent_ref[pl.ds(owner, 1), :], 0.0
         )
         for field in range(fields_count):
-            part = by_column[field * rows : (field + 1) * rows]
-            picked = jnp.sum(jnp.where(row_hot, part, 0.0), axis=0, keepdims=True)
+            chosen = jnp.zeros((8, slots), jnp.float32)
+            for tile in range(rows // 8):
+                start = field * rows + tile * 8
+                chosen = jnp.where(masks[tile], by_column[start : start + 8], chosen)
+            picked = jnp.sum(chosen, axis=0, keepdims=True)
             out_ref[field, pl.ds(owner, 1), :] = picked * weight
 
 
@@ -117,8 +121,8 @@
 def spread_kernel(value_ref, target_ref, out_ref):
     fields_count = value_ref.shape[0]
     slots = value_ref.shape[2]
-    lows = out_ref.shape[1]
-    highs = out_ref.shape[0] // fields_count
+    lows = out_ref.shape[0]
+    highs = out_ref.shape[1] // (2 * fields_count)
 
     @pl.when(pl.program_id(0) == 0)
     def _():
@@ -131,35 +135,40 @@
         target = target_ref[pl.ds(sender, 1), :]
         high_hot = high_ids == target // lows
         low_hot = (low_ids == target % lows).astype(jnp.bfloat16)
+        pieces = []
+        for field in range(fields_count):
+            high, low_part = split_pieces(value_ref[field, pl.ds(sender, 1), :])
+            pieces.append((high, low_part))
         weighted = jnp.concatenate(
             [
-                jnp.where(high_hot, value_ref[field, pl.ds(sender, 1), :], 0.0)
+                jnp.where(high_hot, pieces[field][part].astype(jnp.float32), 0.0).astype(jnp.bfloat16)
+                for part in range(2)
                 for field in range(fields_count)
             ],
             axis=0,
         )
-        for piece in split_pieces(weighted):
-            total = total + lax.dot_general(
-                piece, low_hot, (((1,), (1,)), ((), ())), preferred_element_type=jnp.float32
-            )
+        total = total + lax.dot_general(
+            low_hot, weighted, (((1,), (1,)), ((), ())), preferred_element_type=jnp.float32
+        )
     out_ref[...] += total
 
 
 def spread_cells(values, targets, cells):
     fields_count, senders, slots = values.shape
-    lows = 256
+    lows = 128
     highs = cells // lows
     summed = pl.pallas_call(
         spread_kernel,
-        out_shape=jax.ShapeDtypeStruct((fields_count * highs, lows), jnp.float32),
+        out_shape=jax.ShapeDtypeStruct((lows, 2 * fields_count * highs), jnp.float32),
         grid=(senders // GROUP,),
         in_specs=[
             pl.BlockSpec((fields_count, GROUP, slots), lambda i: (0, i, 0)),
             pl.BlockSpec((GROUP, slots), lambda i: (i, 0)),
         ],
-        out_specs=pl.BlockSpec((fields_count * highs, lows), lambda i: (0, 0)),
+        out_specs=pl.BlockSpec((lows, 2 * fields_count * highs), lambda i: (0, 0)),
     )(values, targets)
-    return summed.reshape(fields_count, cells)
+    summed = summed.reshape(lows, 2, fields_count, highs).sum(axis=1)
+    return jnp.transpose(summed, (1, 2, 0)).reshape(fields_count, cells)
 
 
 def local(

time: 158 us -> 135 us (0.85)
  Pallas kernels: 74.9 us -> 52.1 us
    pallas_call x1, Pallas kernels: 46.4 us -> 26.8 us  [spread_cells(): pl.pallas_call(spread_kernel, out_shape=jax.ShapeDtypeStruct((lows, 2 * f...]
    pallas_call x1, Pallas kernels: 28.5 us -> 25.3 us  [pick_cells(): pl.pallas_call(pick_kernel, out_shape=jax.ShapeDtypeStruct((fields_count,...]
where the time goes in v3:
time: 135 us; the launch traced here: 134 us
  Pallas kernels  52.1 us (39%)
  waiting for transfers between devices  38.1 us (28%)
  starting transfers between devices  24 us (18%)
  local copies, waits for them, and re-layouts  15.4 us (11%)
  other arithmetic  3.65 us (3%)
    all_to_all x1, waiting for transfers between devices, local(): lax.all_to_all(values, ('lat', 'lon'), split_axis=1, concat_axis=1, tiled...  29.5 us
    pallas_call x1, Pallas kernels, spread_cells(): pl.pallas_call(spread_kernel, out_shape=jax.ShapeDtypeStruct((lows, 2 * f...  26.8 us
    pallas_call x1, Pallas kernels, pick_cells(): pl.pallas_call(pick_kernel, out_shape=jax.ShapeDtypeStruct((fields_count,...  25.3 us
    all_to_all x1, starting transfers between devices, local(): lax.all_to_all(values, ('lat', 'lon'), split_axis=1, concat_axis=1, tiled...  13.4 us
    ppermute x1, waiting for transfers between devices, exchange(): from_east = lax.ppermute(block[:, :, :width], 'lon', westward)  4.6 us
    ppermute x1, starting transfers between devices, exchange(): from_west = lax.ppermute(block[:, :, columns - width:], 'lon', eastward)  4.36 us
    pallas_call x1, local copies, waits for them, and re-layouts, pick_cells(): pl.pallas_call(pick_kernel, out_shape=jax.ShapeDtypeStruct((fields_count,...  4.28 us
    ppermute x1, starting transfers between devices, exchange(): from_south = lax.ppermute(top, 'lat', upward)  4.27 us
  transfers between devices with their start and end apart: 6, of which 4 were waited for; matrix products, arithmetic and copies ran while one was open for 2% of the time, Pallas kernels for 0%

profile of v3, /device:TPU:1, one launch (start us, length us, event | category | flops | bytes accessed | tf_op | source)
XLA Modules:
  0.0 134.4 jit_solution(2392508976017337061)
XLA Ops:
  0.6 0.0 copy-start.5
  0.6 0.7 bitcast_dynamic-update-slice_fusion.3
  1.4 0.7 bitcast_dynamic-update-slice_fusion.2
  2.1 0.7 bitcast_dynamic-update-slice_fusion.1
  2.8 0.7 bitcast_dynamic-update-slice_fusion
  3.5 0.9 constant_dynamic-update-slice_fusion
  4.4 0.1 fusion.65
  4.6 4.4 %collective-permute-start = (f32[12,32,8]{2,1,0:T(8,128)S(1)}, f32[12,32,8]{2,1,0:T(8,128)S(1)}, u32[]{:S(2)}, u32[]{:S(2)}) collective-permute-start(f32[12,32,8]{2,1,0:T(8,128)S(1)} %get-tuple-element.22), channel_id=1, source_target_pairs={{0,1},{1,2},{2,3},{3,4},{4,5},{5,6},{6,7},{7,8},{8,9},{9,10},{10,1... | collective-permute-start | bytes 36872 | tf_op jit(solution)/shard_map/ppermute | solution.py:31
  8.9 2.6 %collective-permute-done = f32[12,32,8]{2,1,0:T(8,128)S(1)} collective-permute-done((f32[12,32,8]{2,1,0:T(8,128)S(1)}, f32[12,32,8]{2,1,0:T(8,128)S(1)}, u32[]{:S(2)}, u32[]{:S(2)}) %collective-permute-start) | collective-permute-done | bytes 12320 | tf_op jit(solution)/shard_map/ppermute | solution.py:31
  11.5 4.6 %collective-permute-done.1 = f32[12,32,8]{2,1,0:T(8,128)S(1)} collective-permute-done((f32[12,32,8]{2,1,0:T(8,128)S(1)}, f32[12,32,8]{2,1,0:T(8,128)S(1)}, u32[]{:S(2)}, u32[]{:S(2)}) %collective-permute-start.1) | collective-permute-done | bytes 12320 | tf_op jit(solution)/shard_map/ppermute | solution.py:32
  16.1 0.1 pad_maximum_fusion.6
  16.3 1.3 collective-permute-start.4
  17.6 0.7 collective-permute-start.3
  18.3 0.1 fusion.61
  18.3 0.1 slice.449
  18.4 1.4 %copy.20.tally_ref = s32[128,1]{1,0:T(8,128)} copy(s32[128,1]{0,1:T(1,128)} %bitcast.70) | data formatting | bytes 1024 | tf_op jit(solution)/shard_map/broadcast_in_dim;squeeze | solution.py:118
  19.8 4.3 %collective-permute-start.2 = (f32[12,8,144]{2,1,0:T(8,128)S(1)}, f32[12,8,144]{2,1,0:T(8,128)S(1)}, u32[]{:S(2)}, u32[]{:S(2)}) collective-permute-start(f32[12,8,144]{2,1,0:T(8,128)S(1)} %get-tuple-element.20), channel_id=1, source_target_pairs={{0,16},{16,32},{32,48},{48,64},{64,80},{80,96},{96,112},{1,17},{17... | collective-permute-start | bytes 165896 | tf_op jit(solution)/shard_map/ppermute | solution.py:37
  24.1 0.2 reverse
  24.3 0.1 multiply_select_fusion
  24.4 1.4 %collective-permute-done.2 = f32[12,8,144]{2,1,0:T(8,128)S(1)} collective-permute-done((f32[12,8,144]{2,1,0:T(8,128)S(1)}, f32[12,8,144]{2,1,0:T(8,128)S(1)}, u32[]{:S(2)}, u32[]{:S(2)}) %collective-permute-start.2) | collective-permute-done | bytes 55328 | tf_op jit(solution)/shard_map/ppermute | solution.py:37
  25.8 0.1 multiply_bitcast_fusion
  25.8 0.1 fusion.7
  25.9 0.1 fusion.8
  26.0 0.1 fusion.96
  26.1 0.1 fusion.97
  26.2 0.1 fusion.11
  26.3 0.1 fusion.91
  26.4 0.1 fusion.90
  26.5 0.1 fusion.25
  26.6 0.1 fusion.88
  26.7 0.1 fusion.89
  26.8 0.1 fusion.21
  26.9 0.1 fusion.83
  27.0 0.1 fusion.82
  27.1 0.1 fusion.37
  27.2 0.1 fusion.80
  27.3 0.1 fusion.81
  27.4 0.1 fusion.33
  27.5 0.1 fusion.75
  27.6 0.1 fusion.74
  27.7 0.1 fusion.49
  27.8 0.1 fusion.72
  27.8 0.1 fusion.73
  28.0 0.1 fusion.45
  28.1 0.1 slice_bitcast_fusion
  28.1 0.1 fusion.66
  28.2 0.1 fusion.67
  28.3 0.1 maximum_bitcast_fusion.3
  28.4 0.1 compare_convert_fusion
  28.5 0.1 fusion.53
  28.6 0.1 fusion.55
  28.7 0.0 copy-start.3
  28.7 0.3 compare_select_fusion
  29.0 0.3 fusion.4
  29.4 0.6 pad_maximum_fusion.7
  30.1 25.3 %shard_map.155 = f32[4,128,1024]{2,1,0:T(8,128)} custom-call(f32[128,128]{1,0:T(8,128)} %bitcast.66, s32[128,1024]{1,0:T(8,128)} %bitcast.62, f32[128,1024]{1,0:T(8,128)} %bitcast.63, s32[128,1]{1,0:T(8,128)} %copy.20.tally_ref), custom_call_target="tpu_custom_call" | custom-call | tf_op jit(solution)/shard_map/pallas_call | solution.py:107
  55.4 4.3 %copy.21 = f32[4,128,1024]{2,0,1:T(4,128)} copy(f32[4,128,1024]{2,1,0:T(8,128)} %shard_map.155) | data formatting | bytes 4194304 | tf_op jit(solution)/shard_map/pallas_call | solution.py:107
  59.7 13.4 %all-to-all-start = ((f32[4,128,1024]{2,0,1:T(4,128)}), f32[4,128,1024]{2,0,1:T(4,128)S(1)}, u32[]{:S(2)}, u32[]{:S(2)}) async-start(f32[4,128,1024]{2,0,1:T(4,128)} %copy.21), calls=%async_computation | async-start | bytes 4194304 | tf_op jit(solution)/shard_map/all_to_all | solution.py:249
  73.1 0.7 slice.437
  73.8 29.5 %all-to-all-done = f32[4,128,1024]{2,0,1:T(4,128)S(1)} async-done(((f32[4,128,1024]{2,0,1:T(4,128)}), f32[4,128,1024]{2,0,1:T(4,128)S(1)}, u32[]{:S(2)}, u32[]{:S(2)}) %all-to-all-start) | async-done | bytes 2097184 | tf_op jit(solution)/shard_map/all_to_all | solution.py:249
  103.3 2.6 %copy.22.value_ref = f32[4,128,1024]{2,1,0:T(8,128)} copy(f32[4,128,1024]{2,0,1:T(4,128)S(1)} %all-to-all-done) | data formatting | bytes 4194304 | tf_op jit(solution)/shard_map/all_to_all | solution.py:249
  105.9 26.8 %shard_map.156 = f32[128,256]{1,0:T(8,128)} custom-call(f32[4,128,1024]{2,1,0:T(8,128)} %copy.22.value_ref, s32[128,1024]{1,0:T(8,128)} %bitcast.65), custom_call_target="tpu_custom_call" | custom-call | tf_op jit(solution)/shard_map/pallas_call | solution.py:160
  132.7 1.0 copy.23
  133.7 0.7 copy.26
  (34 shorter events, 0.2 us)
Async XLA Ops:
  0.6 23.6 %copy-start.5 = (f32[12]{0:T(128)S(1)}, f32[12]{0:T(128)}, u32[]{:S(2)}) copy-start(f32[12]{0:T(128)} %constant.55.clone) | copy-start | bytes 148
  4.6 7.0 %collective-permute-start = (f32[12,32,8]{2,1,0:T(8,128)S(1)}, f32[12,32,8]{2,1,0:T(8,128)S(1)}, u32[]{:S(2)}, u32[]{:S(2)}) collective-permute-start(f32[12,32,8]{2,1,0:T(8,128)S(1)} %get-tuple-element.22), channel_id=1, source_target_pairs={{0,1},{1,2},{2,3},{3,4},{4,5},{5,6},{6,7},{7,8},{8,9},{9,10},{10,1... | collective-permute-start | bytes 36872 | tf_op jit(solution)/shard_map/ppermute | solution.py:31
  8.9 7.2 %collective-permute-start.1 = (f32[12,32,8]{2,1,0:T(8,128)S(1)}, f32[12,32,8]{2,1,0:T(8,128)S(1)}, u32[]{:S(2)}, u32[]{:S(2)}) collective-permute-start(f32[12,32,8]{2,1,0:T(8,128)S(1)} %get-tuple-element.23), channel_id=1, source_target_pairs={{1,0},{2,1},{3,2},{4,3},{5,4},{6,5},{7,6},{8,7},{9,8},{10,9},{11,1... | collective-permute-start | bytes 36872 | tf_op jit(solution)/shard_map/ppermute | solution.py:32
  16.3 8.0 %collective-permute-start.4 = (f32[12,8,144]{2,1,0:T(8,128)S(1)}, f32[12,8,144]{2,1,0:T(8,128)S(1)}, u32[]{:S(2)}, u32[]{:S(2)}) collective-permute-start(f32[12,8,144]{2,1,0:T(8,128)S(1)} %get-tuple-element.21), channel_id=1, source_target_pairs={{16,0},{32,16},{48,32},{64,48},{80,64},{96,80},{112,96},{17,1},{33... | collective-permute-start | bytes 165896 | tf_op jit(solution)/shard_map/ppermute | solution.py:38
  17.6 6.5 %collective-permute-start.3 = (f32[12,8,144]{2,1,0:T(8,128)S(1)}, f32[12,8,144]{2,1,0:T(8,128)S(1)}, u32[]{:S(2)}, u32[]{:S(2)}) collective-permute-start(f32[12,8,144]{2,1,0:T(8,128)S(1)} %get-tuple-element.20), channel_id=1, source_target_pairs={{112,127},{113,126},{114,125},{115,124},{116,123},{117,122},{118,1... | collective-permute-start | bytes 165896 | tf_op jit(solution)/shard_map/ppermute | solution.py:41
  19.8 6.0 %collective-permute-start.2 = (f32[12,8,144]{2,1,0:T(8,128)S(1)}, f32[12,8,144]{2,1,0:T(8,128)S(1)}, u32[]{:S(2)}, u32[]{:S(2)}) collective-permute-start(f32[12,8,144]{2,1,0:T(8,128)S(1)} %get-tuple-element.20), channel_id=1, source_target_pairs={{0,16},{16,32},{32,48},{48,64},{64,80},{80,96},{96,112},{1,17},{17... | collective-permute-start | bytes 165896 | tf_op jit(solution)/shard_map/ppermute | solution.py:37
  27.8 1.2 copy-start.1
  27.8 1.2 copy-start.2
  28.7 26.7 %copy-start.3 = (f32[32,128]{1,0:T(8,128)}, f32[32,128]{1,0:T(8,128)S(1)}, u32[]{:S(2)}) copy-start(f32[32,128]{1,0:T(8,128)S(1)} %get-tuple-element.8) | copy-start | bytes 49156
  28.7 26.7 %copy-start.4 = (f32[32,128]{1,0:T(8,128)}, f32[32,128]{1,0:T(8,128)S(1)}, u32[]{:S(2)}) copy-start(f32[32,128]{1,0:T(8,128)S(1)} %get-tuple-element.9) | copy-start | bytes 49156
  29.4 30.3 %copy-start = (f32[8,32,128]{2,1,0:T(8,128)}, f32[8,32,128]{2,1,0:T(8,128)S(1)}, u32[]{:S(2)}) copy-start(f32[8,32,128]{2,1,0:T(8,128)S(1)} %get-tuple-element.5) | copy-start | bytes 393220
  59.7 43.6 %all-to-all-start = ((f32[4,128,1024]{2,0,1:T(4,128)}), f32[4,128,1024]{2,0,1:T(4,128)S(1)}, u32[]{:S(2)}, u32[]{:S(2)}) async-start(f32[4,128,1024]{2,0,1:T(4,128)} %copy.21), calls=%async_computation | async-start | bytes 4194304 | tf_op jit(solution)/shard_map/all_to_all | solution.py:249

commit v4 on v3

--- a/solution.py
+++ b/solution.py
@@ -71,7 +71,7 @@
 
 
 def pick_kernel(table_ref, index_ref, extent_ref, tally_ref, out_ref):
-    fields_count = out_ref.shape[0]
+    fields_count = out_ref.shape[1]
     slots = index_ref.shape[1]
     table_rows = table_ref.shape[0]
     columns = table_ref.shape[1]
@@ -97,7 +97,7 @@
                 start = field * rows + tile * 8
                 chosen = jnp.where(masks[tile], by_column[start : start + 8], chosen)
             picked = jnp.sum(chosen, axis=0, keepdims=True)
-            out_ref[field, pl.ds(owner, 1), :] = picked * weight
+            out_ref[owner, pl.ds(field, 1), :] = picked * weight
 
 
 def pick_cells(surface_grid, indices, extent, tally):
@@ -106,7 +106,7 @@
     table = surface_grid.reshape(fields_count * rows, columns)
     return pl.pallas_call(
         pick_kernel,
-        out_shape=jax.ShapeDtypeStruct((fields_count, owners, slots), jnp.float32),
+        out_shape=jax.ShapeDtypeStruct((owners, fields_count, slots), jnp.float32),
         grid=(owners // GROUP,),
         in_specs=[
             pl.BlockSpec((fields_count * rows, columns), lambda i: (0, 0)),
@@ -114,12 +114,12 @@
             pl.BlockSpec((GROUP, slots), lambda i: (i, 0)),
             pl.BlockSpec((GROUP, 1), lambda i: (i, 0)),
         ],
-        out_specs=pl.BlockSpec((fields_count, GROUP, slots), lambda i: (0, i, 0)),
+        out_specs=pl.BlockSpec((GROUP, fields_count, slots), lambda i: (i, 0, 0)),
     )(table, indices, extent, tally[:, None])
 
 
 def spread_kernel(value_ref, target_ref, out_ref):
-    fields_count = value_ref.shape[0]
+    fields_count = value_ref.shape[1]
     slots = value_ref.shape[2]
     lows = out_ref.shape[0]
     highs = out_ref.shape[1] // (2 * fields_count)
@@ -137,7 +137,7 @@
         low_hot = (low_ids == target % lows).astype(jnp.bfloat16)
         pieces = []
         for field in range(fields_count):
-            high, low_part = split_pieces(value_ref[field, pl.ds(sender, 1), :])
+            high, low_part = split_pieces(value_ref[sender, pl.ds(field, 1), :])
             pieces.append((high, low_part))
         weighted = jnp.concatenate(
             [
@@ -154,7 +154,7 @@
 
 
 def spread_cells(values, targets, cells):
-    fields_count, senders, slots = values.shape
+    senders, fields_count, slots = values.shape
     lows = 128
     highs = cells // lows
     summed = pl.pallas_call(
@@ -162,7 +162,7 @@
         out_shape=jax.ShapeDtypeStruct((lows, 2 * fields_count * highs), jnp.float32),
         grid=(senders // GROUP,),
         in_specs=[
-            pl.BlockSpec((fields_count, GROUP, slots), lambda i: (0, i, 0)),
+            pl.BlockSpec((GROUP, fields_count, slots), lambda i: (i, 0, 0)),
             pl.BlockSpec((GROUP, slots), lambda i: (i, 0)),
         ],
         out_specs=pl.BlockSpec((lows, 2 * fields_count * highs), lambda i: (0, 0)),
@@ -246,7 +246,7 @@
     values = pick_cells(
         surface_grid, sent_sender_mesh_index[0], sent_intersection_extent[0], sent_entry_tally[0]
     )
-    block = lax.all_to_all(values, ("lat", "lon"), split_axis=1, concat_axis=1, tiled=True)
+    block = lax.all_to_all(values, ("lat", "lon"), split_axis=0, concat_axis=0, tiled=True)
     atmosphere = spread_cells(block, received_atmosphere_mesh_index[0], ACELL)
     return (height, east, north, tracer_new, atmosphere)
 

time: 135 us -> 129 us (0.956)
  local copies, waits for them, and re-layouts: 15.4 us -> 9.93 us
    pallas_call x1 -> x0, local copies, waits for them, and re-layouts: 4.28 us -> none  [pick_cells(): pl.pallas_call(pick_kernel, out_shape=jax.ShapeDtypeStruct((fields_count,...]
    all_to_all x1 -> x0, local copies, waits for them, and re-layouts: 2.56 us -> none  [local(): lax.all_to_all(values, ('lat', 'lon'), split_axis=1, concat_axis=1, tiled...]
    unnamed x17 -> x19, local copies, waits for them, and re-layouts: 3.05 us -> 4.39 us
where the time goes in v4:
time: 129 us
  Pallas kernels  51.9 us (40%)
  waiting for transfers between devices  38.1 us (30%)
  starting transfers between devices  24 us (19%)
  local copies, waits for them, and re-layouts  9.93 us (8%)
  other arithmetic  3.65 us (3%)
    all_to_all x1, waiting for transfers between devices, local(): lax.all_to_all(values, ('lat', 'lon'), split_axis=0, concat_axis=0, tiled...  29.5 us
    pallas_call x1, Pallas kernels, spread_cells(): pl.pallas_call(spread_kernel, out_shape=jax.ShapeDtypeStruct((lows, 2 * f...  26.6 us
    pallas_call x1, Pallas kernels, pick_cells(): pl.pallas_call(pick_kernel, out_shape=jax.ShapeDtypeStruct((owners, field...  25.3 us
    all_to_all x1, starting transfers between devices, local(): lax.all_to_all(values, ('lat', 'lon'), split_axis=0, concat_axis=0, tiled...  13.4 us
    ppermute x1, waiting for transfers between devices, exchange(): from_east = lax.ppermute(block[:, :, :width], 'lon', westward)  4.6 us
    unnamed x19, local copies, waits for them, and re-layouts  4.39 us
    ppermute x1, starting transfers between devices, exchange(): from_west = lax.ppermute(block[:, :, columns - width:], 'lon', eastward)  4.36 us
    ppermute x1, starting transfers between devices, exchange(): from_south = lax.ppermute(top, 'lat', upward)  4.27 us
  transfers between devices with their start and end apart: 6, of which 4 were waited for; matrix products, arithmetic and copies ran while one was open for 2% of the time, Pallas kernels for 0%

profile of v4, /device:TPU:1, one launch (start us, length us, event | category | flops | bytes accessed | tf_op | source)
XLA Modules:
  0.0 128.6 jit_solution(971861925514400815)
XLA Ops:
  0.6 0.0 copy-start.6
  0.6 0.7 bitcast_dynamic-update-slice_fusion.3
  1.4 0.7 bitcast_dynamic-update-slice_fusion.2
  2.1 0.7 bitcast_dynamic-update-slice_fusion.1
  2.8 0.7 bitcast_dynamic-update-slice_fusion
  3.5 0.9 constant_dynamic-update-slice_fusion
  4.4 0.1 fusion.65
  4.6 4.4 %collective-permute-start = (f32[12,32,8]{2,1,0:T(8,128)S(1)}, f32[12,32,8]{2,1,0:T(8,128)S(1)}, u32[]{:S(2)}, u32[]{:S(2)}) collective-permute-start(f32[12,32,8]{2,1,0:T(8,128)S(1)} %get-tuple-element.22), channel_id=1, source_target_pairs={{0,1},{1,2},{2,3},{3,4},{4,5},{5,6},{6,7},{7,8},{8,9},{9,10},{10,1... | collective-permute-start | bytes 36872 | tf_op jit(solution)/shard_map/ppermute | solution.py:31
  8.9 2.6 %collective-permute-done = f32[12,32,8]{2,1,0:T(8,128)S(1)} collective-permute-done((f32[12,32,8]{2,1,0:T(8,128)S(1)}, f32[12,32,8]{2,1,0:T(8,128)S(1)}, u32[]{:S(2)}, u32[]{:S(2)}) %collective-permute-start) | collective-permute-done | bytes 12320 | tf_op jit(solution)/shard_map/ppermute | solution.py:31
  11.5 4.6 %collective-permute-done.1 = f32[12,32,8]{2,1,0:T(8,128)S(1)} collective-permute-done((f32[12,32,8]{2,1,0:T(8,128)S(1)}, f32[12,32,8]{2,1,0:T(8,128)S(1)}, u32[]{:S(2)}, u32[]{:S(2)}) %collective-permute-start.1) | collective-permute-done | bytes 12320 | tf_op jit(solution)/shard_map/ppermute | solution.py:32
  16.1 0.1 pad_maximum_fusion.6
  16.3 1.3 %collective-permute-start.4 = (f32[12,8,144]{2,1,0:T(8,128)S(1)}, f32[12,8,144]{2,1,0:T(8,128)S(1)}, u32[]{:S(2)}, u32[]{:S(2)}) collective-permute-start(f32[12,8,144]{2,1,0:T(8,128)S(1)} %get-tuple-element.21), channel_id=1, source_target_pairs={{16,0},{32,16},{48,32},{64,48},{80,64},{96,80},{112,96},{17,1},{33... | collective-permute-start | bytes 165896 | tf_op jit(solution)/shard_map/ppermute | solution.py:38
  17.6 0.7 collective-permute-start.3
  18.3 0.1 fusion.61
  18.3 0.1 slice.449
  18.4 1.4 %copy.18.tally_ref = s32[128,1]{1,0:T(8,128)} copy(s32[128,1]{0,1:T(1,128)} %bitcast.70) | data formatting | bytes 1024 | tf_op jit(solution)/shard_map/broadcast_in_dim;squeeze | solution.py:118
  19.8 4.3 %collective-permute-start.2 = (f32[12,8,144]{2,1,0:T(8,128)S(1)}, f32[12,8,144]{2,1,0:T(8,128)S(1)}, u32[]{:S(2)}, u32[]{:S(2)}) collective-permute-start(f32[12,8,144]{2,1,0:T(8,128)S(1)} %get-tuple-element.20), channel_id=1, source_target_pairs={{0,16},{16,32},{32,48},{48,64},{64,80},{80,96},{96,112},{1,17},{17... | collective-permute-start | bytes 165896 | tf_op jit(solution)/shard_map/ppermute | solution.py:37
  24.1 0.2 reverse
  24.3 0.1 multiply_select_fusion
  24.4 1.4 %collective-permute-done.2 = f32[12,8,144]{2,1,0:T(8,128)S(1)} collective-permute-done((f32[12,8,144]{2,1,0:T(8,128)S(1)}, f32[12,8,144]{2,1,0:T(8,128)S(1)}, u32[]{:S(2)}, u32[]{:S(2)}) %collective-permute-start.2) | collective-permute-done | bytes 55328 | tf_op jit(solution)/shard_map/ppermute | solution.py:37
  25.8 0.1 multiply_bitcast_fusion
  25.8 0.1 fusion.7
  25.9 0.1 fusion.8
  26.0 0.1 fusion.96
  26.1 0.1 fusion.97
  26.2 0.1 fusion.11
  26.3 0.1 fusion.91
  26.4 0.1 fusion.90
  26.5 0.1 fusion.25
  26.6 0.1 fusion.88
  26.7 0.1 fusion.89
  26.8 0.1 fusion.21
  26.9 0.1 fusion.83
  27.0 0.1 fusion.82
  27.1 0.1 fusion.37
  27.2 0.1 fusion.80
  27.3 0.1 fusion.81
  27.4 0.1 fusion.33
  27.5 0.1 fusion.75
  27.6 0.1 fusion.74
  27.7 0.1 fusion.49
  27.8 0.1 fusion.72
  27.8 0.1 fusion.73
  28.0 0.1 fusion.45
  28.1 0.1 slice_bitcast_fusion
  28.1 0.1 fusion.66
  28.2 0.1 fusion.67
  28.3 0.1 maximum_bitcast_fusion.3
  28.4 0.1 compare_convert_fusion
  28.5 0.1 fusion.53
  28.6 0.1 fusion.55
  28.7 0.0 copy-start.4
  28.7 0.0 copy-start.5
  28.7 0.3 compare_select_fusion
  29.0 0.3 fusion.4
  29.4 0.6 pad_maximum_fusion.7
  30.1 25.3 %shard_map.155 = f32[128,4,1024]{2,1,0:T(4,128)} custom-call(f32[128,128]{1,0:T(8,128)} %bitcast.66, s32[128,1024]{1,0:T(8,128)} %bitcast.62, f32[128,1024]{1,0:T(8,128)} %bitcast.63, s32[128,1]{1,0:T(8,128)} %copy.18.tally_ref), custom_call_target="tpu_custom_call" | custom-call | tf_op jit(solution)/shard_map/pallas_call | solution.py:107
  55.4 13.4 %all-to-all-start = ((f32[128,4,1024]{2,1,0:T(4,128)}), f32[128,4,1024]{2,1,0:T(4,128)S(1)}, u32[]{:S(2)}, u32[]{:S(2)}) async-start(f32[128,4,1024]{2,1,0:T(4,128)} %shard_map.155), calls=%async_computation | async-start | bytes 4194304 | tf_op jit(solution)/shard_map/all_to_all | solution.py:249
  68.8 0.7 slice.437
  69.5 29.5 %all-to-all-done.value_ref = f32[128,4,1024]{2,1,0:T(4,128)S(1)} async-done(((f32[128,4,1024]{2,1,0:T(4,128)}), f32[128,4,1024]{2,1,0:T(4,128)S(1)}, u32[]{:S(2)}, u32[]{:S(2)}) %all-to-all-start) | async-done | bytes 2097184 | tf_op jit(solution)/shard_map/all_to_all | solution.py:249
  99.0 1.3 %copy-done = f32[128,4,1024]{2,1,0:T(4,128)} copy-done((f32[128,4,1024]{2,1,0:T(4,128)}, f32[128,4,1024]{2,1,0:T(4,128)S(1)}, u32[]{:S(2)}) %copy-start) | copy-done | bytes 2097176
  100.3 26.6 %shard_map.156 = f32[128,256]{1,0:T(8,128)} custom-call(f32[128,4,1024]{2,1,0:T(4,128)} %copy-done, s32[128,1024]{1,0:T(8,128)} %bitcast.65), custom_call_target="tpu_custom_call" | custom-call | tf_op jit(solution)/shard_map/pallas_call | solution.py:160
  126.9 1.0 copy.19
  127.9 0.7 copy.22
  (34 shorter events, 0.2 us)
Async XLA Ops:
  0.6 23.6 %copy-start.6 = (f32[12]{0:T(128)S(1)}, f32[12]{0:T(128)}, u32[]{:S(2)}) copy-start(f32[12]{0:T(128)} %constant.55.clone) | copy-start | bytes 148
  4.6 7.0 %collective-permute-start = (f32[12,32,8]{2,1,0:T(8,128)S(1)}, f32[12,32,8]{2,1,0:T(8,128)S(1)}, u32[]{:S(2)}, u32[]{:S(2)}) collective-permute-start(f32[12,32,8]{2,1,0:T(8,128)S(1)} %get-tuple-element.22), channel_id=1, source_target_pairs={{0,1},{1,2},{2,3},{3,4},{4,5},{5,6},{6,7},{7,8},{8,9},{9,10},{10,1... | collective-permute-start | bytes 36872 | tf_op jit(solution)/shard_map/ppermute | solution.py:31
  8.9 7.2 %collective-permute-start.1 = (f32[12,32,8]{2,1,0:T(8,128)S(1)}, f32[12,32,8]{2,1,0:T(8,128)S(1)}, u32[]{:S(2)}, u32[]{:S(2)}) collective-permute-start(f32[12,32,8]{2,1,0:T(8,128)S(1)} %get-tuple-element.23), channel_id=1, source_target_pairs={{1,0},{2,1},{3,2},{4,3},{5,4},{6,5},{7,6},{8,7},{9,8},{10,9},{11,1... | collective-permute-start | bytes 36872 | tf_op jit(solution)/shard_map/ppermute | solution.py:32
  16.3 8.0 %collective-permute-start.4 = (f32[12,8,144]{2,1,0:T(8,128)S(1)}, f32[12,8,144]{2,1,0:T(8,128)S(1)}, u32[]{:S(2)}, u32[]{:S(2)}) collective-permute-start(f32[12,8,144]{2,1,0:T(8,128)S(1)} %get-tuple-element.21), channel_id=1, source_target_pairs={{16,0},{32,16},{48,32},{64,48},{80,64},{96,80},{112,96},{17,1},{33... | collective-permute-start | bytes 165896 | tf_op jit(solution)/shard_map/ppermute | solution.py:38
  17.6 6.5 %collective-permute-start.3 = (f32[12,8,144]{2,1,0:T(8,128)S(1)}, f32[12,8,144]{2,1,0:T(8,128)S(1)}, u32[]{:S(2)}, u32[]{:S(2)}) collective-permute-start(f32[12,8,144]{2,1,0:T(8,128)S(1)} %get-tuple-element.20), channel_id=1, source_target_pairs={{112,127},{113,126},{114,125},{115,124},{116,123},{117,122},{118,1... | collective-permute-start | bytes 165896 | tf_op jit(solution)/shard_map/ppermute | solution.py:41
  19.8 6.0 %collective-permute-start.2 = (f32[12,8,144]{2,1,0:T(8,128)S(1)}, f32[12,8,144]{2,1,0:T(8,128)S(1)}, u32[]{:S(2)}, u32[]{:S(2)}) collective-permute-start(f32[12,8,144]{2,1,0:T(8,128)S(1)} %get-tuple-element.20), channel_id=1, source_target_pairs={{0,16},{16,32},{32,48},{48,64},{64,80},{80,96},{96,112},{1,17},{17... | collective-permute-start | bytes 165896 | tf_op jit(solution)/shard_map/ppermute | solution.py:37
  27.8 1.2 copy-start.2
  27.8 1.2 copy-start.3
  28.7 26.6 %copy-start.4 = (f32[32,128]{1,0:T(8,128)}, f32[32,128]{1,0:T(8,128)S(1)}, u32[]{:S(2)}) copy-start(f32[32,128]{1,0:T(8,128)S(1)} %get-tuple-element.8) | copy-start | bytes 49156
  28.7 26.6 %copy-start.5 = (f32[32,128]{1,0:T(8,128)}, f32[32,128]{1,0:T(8,128)S(1)}, u32[]{:S(2)}) copy-start(f32[32,128]{1,0:T(8,128)S(1)} %get-tuple-element.9) | copy-start | bytes 49156
  29.4 26.0 %copy-start.1 = (f32[8,32,128]{2,1,0:T(8,128)}, f32[8,32,128]{2,1,0:T(8,128)S(1)}, u32[]{:S(2)}) copy-start(f32[8,32,128]{2,1,0:T(8,128)S(1)} %get-tuple-element.5) | copy-start | bytes 393220
  55.4 43.6 %all-to-all-start = ((f32[128,4,1024]{2,1,0:T(4,128)}), f32[128,4,1024]{2,1,0:T(4,128)S(1)}, u32[]{:S(2)}, u32[]{:S(2)}) async-start(f32[128,4,1024]{2,1,0:T(4,128)} %shard_map.155), calls=%async_computation | async-start | bytes 4194304 | tf_op jit(solution)/shard_map/all_to_all | solution.py:249
  99.0 1.3 %copy-start = (f32[128,4,1024]{2,1,0:T(4,128)}, f32[128,4,1024]{2,1,0:T(4,128)S(1)}, u32[]{:S(2)}) copy-start(f32[128,4,1024]{2,1,0:T(4,128)S(1)} %all-to-all-done.value_ref) | copy-start | bytes 6291460
